TPU v7x, 256 devices: a whole 4x4x8 slice. The times are simulated.
256 devices in a mesh: section: 4 (over x), rows: 16 (over z_lo, y, core), dp: 4 (over z_hi).
Axes of the slice: x: 4, y: 4, z: 8 (z_hi: 4, z_lo: 2; z = z_hi * 2 + z_lo), core: 2. Of those that a mesh axis runs over, the one named last changes fastest.
Arguments:
- latent: bfloat16 [8, 2, 64, 8, 192], P('dp', None, 'rows'), may hold values from -6 to 6
- enc_weight: bfloat16 [4, 5184, 192], P('section'), may hold values from -0.078125 to 0.078125
- dec_weight: bfloat16 [4, 5184, 192], P('section'), may hold values from -0.078125 to 0.078125
- enc_gain: float32 [4, 192], P('section'), may hold values from 0.1 to 1.9
- dec_gain: float32 [4, 192], P('section'), may hold values from 0.1 to 1.9
- out_grad: bfloat16 [8, 2, 64, 8, 192], P('dp', None, 'rows'), may hold values from -6 to 6
Outputs:
- enc_wgrad: float32 [4, 5184, 192], P('section', ('rows', 'dp'))
- dec_wgrad: float32 [4, 5184, 192], P('section', ('rows', 'dp'))
- enc_ggrad: float32 [4, 192], P('section', ('rows', 'dp'))
- dec_ggrad: float32 [4, 192], P('section', ('rows', 'dp'))
All inputs are finite; a program needn't handle non-finite values.
Results may differ from a plain program's by a relative error of at most 0.028.
Values may be sent and summed in bfloat16 or wider, within the bound.
No kernel may reach another device: no remote copies, remote signals or barrier semaphores. Data moves between devices by JAX's collectives and lax.ppermute only.
A program may use at most 128 MiB of HBM per device.

v0:
```python
import math

import jax
import jax.numpy as jnp
from jax import lax
from jax.sharding import PartitionSpec as P

GROUPS = 32


EPSILON = 1e-05


def spread_groups(values, channels):
    return jnp.repeat(values, channels // GROUPS, axis=-1)[:, None, None, None, :]


def rows_allsum(value):
    count = lax.axis_size("rows")
    if count & (count - 1):
        return lax.psum(value, "rows")
    mask = 1
    while mask < count:
        partner = [(i, i ^ mask) for i in range(count)]
        value = value + lax.ppermute(value, "rows", partner)
        mask *= 2
    return value


def rows_gather(value):
    count = lax.axis_size("rows")
    slots = jnp.zeros((count,) + value.shape, value.dtype)
    slots = lax.dynamic_update_index_in_dim(slots, value, lax.axis_index("rows"), 0)
    return rows_allsum(slots)


def edge_rows(block):
    count = lax.axis_size("rows")
    up = [(i, i + 1) for i in range(count - 1)]
    down = [(i + 1, i) for i in range(count - 1)]
    low = lax.ppermute(block[:, :, -1:], "rows", up)
    high = lax.ppermute(block[:, :, :1], "rows", down)
    return low, high


def gather_patches(grown_rows):
    frames, padded_rows, columns, channels = grown_rows.shape
    inner_rows = padded_rows - 2
    padded = jnp.pad(grown_rows, ((1, 1), (0, 0), (1, 1), (0, 0)))
    pieces = []
    for lag_frame in range(3):
        for lag_row in range(3):
            for lag_column in range(3):
                pieces.append(
                    padded[
                        lag_frame : lag_frame + frames,
                        lag_row : lag_row + inner_rows,
                        lag_column : lag_column + columns,
                        :,
                    ]
                )
    return jnp.concatenate(pieces, axis=-1).reshape(frames * inner_rows * columns, 27 * channels)


def conv_rows(grown, weights):
    batches, frames, grown_rows, columns, _ = grown.shape
    patches = jax.vmap(gather_patches)(grown).reshape(-1, weights.shape[0])
    out = jnp.dot(patches, weights, preferred_element_type=jnp.float32)
    return out.reshape(batches, frames, grown_rows - 2, columns, weights.shape[1])


def flipped(weights):
    channels = weights.shape[1]
    blocks = weights.reshape(27, -1, channels)[::-1]
    return jnp.swapaxes(blocks, 1, 2).reshape(-1, blocks.shape[1])


def with_halo(low, own, high, keep_low, keep_high):
    low = jnp.where(keep_low, low, jnp.zeros_like(low))
    high = jnp.where(keep_high, high, jnp.zeros_like(high))
    return jnp.concatenate([low, own, high], axis=2)


def forward_block(volume, gain_vec, weights, counted, keep_low, keep_high):
    batches = volume.shape[0]
    channels = volume.shape[-1]
    local_count = counted // lax.axis_size("rows")
    grouped = volume.reshape(batches, -1, GROUPS, channels // GROUPS)
    local_sum = jnp.sum(grouped, axis=(1, 3))
    local_mean = local_sum / local_count
    deviation = grouped - local_mean[:, None, :, None]
    local_sq = jnp.sum(deviation * deviation, axis=(1, 3))
    low, high = edge_rows(volume)
    gathered = rows_gather(jnp.stack([local_sum, local_sq]))
    sums = gathered[:, 0]
    squares = gathered[:, 1]
    centre = jnp.sum(sums, axis=0) / counted
    part_means = sums / local_count
    spread = (
        jnp.sum(squares, axis=0) + local_count * jnp.sum((part_means - centre) ** 2, axis=0)
    ) / counted
    inverse = lax.rsqrt(spread + EPSILON)
    full = jnp.concatenate([low, volume, high], axis=2)
    normed = (full - spread_groups(centre, channels)) * spread_groups(inverse, channels)
    active = jax.nn.silu(normed * gain_vec).astype(jnp.bfloat16)
    active = with_halo(active[:, :, :1], active[:, :, 1:-1], active[:, :, -1:], keep_low, keep_high)
    result = volume + conv_rows(active, weights)
    return active, centre, inverse, result


def backward_block(volume, gain_vec, reverse_weights, centre, inverse, cot, counted, keep_low, keep_high):
    channels = volume.shape[-1]
    batches = volume.shape[0]
    inverse_full = spread_groups(inverse, channels)
    normed = (volume - spread_groups(centre, channels)) * inverse_full
    zvalue = normed * gain_vec
    cot_low = cot.astype(jnp.bfloat16)
    act_grad = conv_rows(cot_low, reverse_weights)
    logistic = jax.nn.sigmoid(zvalue)
    pre_grad = act_grad * logistic * (1.0 + zvalue * (1.0 - logistic))
    hat_grad = pre_grad * gain_vec
    grouped_grad = hat_grad.reshape(batches, -1, GROUPS, channels // GROUPS)
    grouped_hat = normed.reshape(batches, -1, GROUPS, channels // GROUPS)
    halo_low, halo_high = edge_rows(jnp.concatenate([hat_grad, normed], axis=-1))
    sums = rows_allsum(
        jnp.stack([jnp.sum(grouped_grad, axis=(1, 3)), jnp.sum(grouped_grad * grouped_hat, axis=(1, 3))])
    )
    first = spread_groups(sums[0] / counted, channels)
    second = spread_groups(sums[1] / counted, channels)
    grad_full = jnp.concatenate([halo_low[..., :channels], hat_grad, halo_high[..., :channels]], axis=2)
    hat_full = jnp.concatenate([halo_low[..., channels:], normed, halo_high[..., channels:]], axis=2)
    passed = cot + inverse_full * (grad_full - first - hat_full * second)
    passed = with_halo(passed[:, :, :1], passed[:, :, 1:-1], passed[:, :, -1:], keep_low, keep_high)
    gain_part = jnp.sum((pre_grad * normed).reshape(-1, channels), axis=0)
    return passed, cot_low[:, :, 1:-1], gain_part


def weight_gradient(grown, cot_low):
    patches = jax.vmap(gather_patches)(grown)
    patches = patches.reshape(-1, patches.shape[-1])
    flat_cot = cot_low.reshape(-1, cot_low.shape[-1])
    return lax.dot_general(
        patches, flat_cot, (((0,), (0,)), ((), ())), preferred_element_type=jnp.float32
    )


def reduced_grads(weight_grad, gain_grad, form, after=None):
    shards = lax.axis_size("rows") * lax.axis_size("dp")
    rows_out = weight_grad.shape[0] // shards
    gains_out = gain_grad.shape[0] // shards
    position = lax.axis_index("rows") * lax.axis_size("dp") + lax.axis_index("dp")
    packed = jnp.concatenate(
        [weight_grad.reshape(shards, -1), gain_grad.reshape(shards, gains_out)], axis=1
    )
    if after is not None:
        packed = packed + 0.0 * after[:1, :1]
    if form == "sum":
        total = lax.dynamic_index_in_dim(lax.psum(packed, ("rows", "dp")), position, 0, keepdims=False)
    else:
        total = lax.psum_scatter(packed, ("rows", "dp"), scatter_dimension=0, tiled=True)[0]
    split = rows_out * weight_grad.shape[1]
    return total[:split].reshape(rows_out, weight_grad.shape[1]), total[split:], packed[0, 0]


def on_device(latent, enc_weight, dec_weight, enc_gain, dec_gain, out_grad):
    section_pos = lax.axis_index("section")
    rows_pos = lax.axis_index("rows")
    keep_low = rows_pos > 0
    keep_high = rows_pos < lax.axis_size("rows") - 1
    batches, frames, rows_here, columns, channels = latent.shape
    levels = lax.axis_size("section")
    counted = frames * rows_here * columns * (channels // GROUPS) * lax.axis_size("rows")
    cells_all = batches * lax.axis_size("dp") * frames * rows_here * lax.axis_size("rows") * columns
    loss_scale = 1.0 / math.sqrt(cells_all)
    enc_all = lax.all_gather(enc_weight[0], "section")
    dec_all = lax.all_gather(dec_weight[0], "section")
    enc_gains = lax.all_gather(enc_gain[0], "section")
    dec_gains = lax.all_gather(dec_gain[0], "section")

    hidden = latent.astype(jnp.float32)
    enc_inputs = []
    enc_active = []
    enc_stats = []
    for level in range(levels):
        enc_inputs.append(hidden)
        active, centre, inverse, result = forward_block(
            hidden, enc_gains[level], enc_all[level], counted, keep_low, keep_high
        )
        enc_active.append(active)
        enc_stats.append((centre, inverse))
        hidden = result.astype(jnp.bfloat16).astype(jnp.float32)
    dec_inputs = [None] * levels
    dec_active = [None] * levels
    dec_stats = [None] * levels
    coming = hidden
    for level in reversed(range(levels)):
        united = coming + enc_inputs[level]
        dec_inputs[level] = united
        active, centre, inverse, result = forward_block(
            united, dec_gains[level], dec_all[level], counted, keep_low, keep_high
        )
        dec_active[level] = active
        dec_stats[level] = (centre, inverse)
        coming = result.astype(jnp.bfloat16).astype(jnp.float32)

    seeded_low, seeded_high = edge_rows(out_grad)
    cot = with_halo(seeded_low, out_grad, seeded_high, keep_low, keep_high).astype(jnp.float32) * loss_scale
    skip_grads = [None] * levels
    dec_cots = [None] * levels
    dec_gain_parts = [None] * levels
    for level in range(levels):
        cot, cot_low, gain_part = backward_block(
            dec_inputs[level],
            dec_gains[level],
            flipped(dec_all[level]),
            dec_stats[level][0],
            dec_stats[level][1],
            cot,
            counted,
            keep_low,
            keep_high,
        )
        skip_grads[level] = cot
        dec_cots[level] = cot_low
        dec_gain_parts[level] = gain_part
    own_dec = weight_gradient(
        lax.dynamic_index_in_dim(jnp.stack(dec_active), section_pos, 0, keepdims=False),
        lax.dynamic_index_in_dim(jnp.stack(dec_cots), section_pos, 0, keepdims=False),
    )
    dec_gain_own = lax.dynamic_index_in_dim(jnp.stack(dec_gain_parts), section_pos, 0, keepdims=False)
    dec_result, dec_gains_out, _ = reduced_grads(own_dec, dec_gain_own, "sum")

    enc_cots = [None] * levels
    enc_gain_parts = [None] * levels
    for level in reversed(range(levels)):
      passed, cot_low, gain_part = backward_block(
          enc_inputs[level],
          enc_gains[level],
          flipped(enc_all[level]),
          enc_stats[level][0],
          enc_stats[level][1],
          cot,
          counted,
          keep_low,
          keep_high,
      )
      cot = passed + skip_grads[level]
      enc_cots[level] = cot_low
      enc_gain_parts[level] = gain_part
    late_pos = section_pos + (0.0 * dec_result[0, 0]).astype(section_pos.dtype)
    own_enc = weight_gradient(
        lax.dynamic_index_in_dim(jnp.stack(enc_active), late_pos, 0, keepdims=False),
        lax.dynamic_index_in_dim(jnp.stack(enc_cots), late_pos, 0, keepdims=False),
    )
    enc_gain_own = lax.dynamic_index_in_dim(jnp.stack(enc_gain_parts), late_pos, 0, keepdims=False)
    enc_result, enc_gains_out, _ = reduced_grads(own_enc, enc_gain_own, "scatter", dec_result)
    return (enc_result[None], dec_result[None], enc_gains_out[None], dec_gains_out[None])


def solution(mesh):
    in_specs = (
        P("dp", None, "rows", None, None),
        P("section", None, None),
        P("section", None, None),
        P("section", None),
        P("section", None),
        P("dp", None, "rows", None, None),
    )
    out_specs = (
        P("section", ("rows", "dp"), None),
        P("section", ("rows", "dp"), None),
        P("section", ("rows", "dp")),
        P("section", ("rows", "dp")),
    )

    return jax.shard_map(on_device, mesh=mesh, in_specs=in_specs, out_specs=out_specs, check_vma=False)
```

profile of v0, /device:TPU:6, one launch (start us, length us, event | category | flops | bytes accessed | tf_op | source)
XLA Modules:
  0.0 1050.0 jit_solution(276224755303149563)
XLA Ops:
  22.3 6.7 all-gather
  29.1 7.3 collective-permute-start.5
  40.7 53.7 %all-gather.5.cloned.1.call-done = bf16[4,5184,192]{1,2,0:T(8,128)(2,1)} async-done(((bf16[1,5184,192]{1,2,0:T(8,128)(2,1)}), bf16[4,5184,192]{1,2,0:T(8,128)(2,1)}) %all-gather.5.cloned.1.call-update) | async-done | bytes 7962640 | tf_op jit(solution)/shard_map/all_gather | solution.py:175
  156.2 4.0 collective-permute-start.22
  181.1 3.6 collective-permute-start.48
  184.7 7.4 all-gather.1
  201.7 4.1 collective-permute-start.29
  221.5 3.4 collective-permute-done.33
  224.9 4.4 collective-permute-start.34
  252.6 6.2 fusion.240
  259.4 4.4 collective-permute-start.40
  267.1 3.8 copy.127
  285.3 3.7 concatenate.268
  289.1 4.0 fusion.272
  308.0 3.8 copy.77
  316.6 3.8 copy.80
  321.9 4.0 collective-permute-start.46
  327.6 3.8 copy.84
  334.8 4.6 copy.75
  339.3 3.8 copy.87
  351.1 3.9 multiply_reduce_fusion.10
  363.5 4.6 copy.78
  368.1 3.8 copy.90
  385.2 4.3 collective-permute-start.55
  401.3 3.8 concatenate.278
  405.0 3.9 multiply_reduce_fusion.9
  419.8 3.8 copy.93
  427.5 4.5 copy.81
  432.0 3.8 copy.97
  436.6 6.2 collective-permute-start.60
  456.7 3.8 concatenate.283
  460.5 3.9 multiply_reduce_fusion.8
  475.7 4.7 copy.85
  483.7 4.6 copy.91
  491.8 4.6 copy.98
  501.4 4.8 collective-permute-start.66
  530.2 3.5 collective-permute-start.72
  557.8 3.5 collective-permute-start.78
  587.0 3.6 collective-permute-start.84
  599.9 3.5 concatenate.305
  612.6 5.8 reshape.338
  622.1 4.5 collective-permute-start.90
  626.6 4.3 pad_maximum_fusion
  639.1 3.7 concatenate.310
  644.9 181.6 %all-reduce.21.cloned.1.call-done = f32[64,15555]{1,0:T(8,128)} async-done(((f32[64,15555]{1,0:T(8,128)}), f32[64,15555]{1,0:T(8,128)}) %all-reduce.21.cloned.1.call-update) | async-done | bytes 3982096 | tf_op jit(solution)/shard_map/psum | solution.py:158
  833.6 5.7 reshape.347
  839.5 4.3 maximum_add_fusion
  847.1 191.6 %all-reduce.23.cloned.1.call-done = f32[64,15555]{1,0:T(8,128)} async-done(((f32[64,15555]{1,0:T(8,128)}), f32[64,15555]{1,0:T(8,128)}) %all-reduce.23.cloned.1.call-update) | async-done | bytes 3982096
  (781 shorter events, 407.1 us)
Async XLA Ops:
  7.2 87.2 %all-gather.5.cloned.1.call-start = ((), (), s32[]{:S(2)}) async-start(), calls=%async_computation | async-start | bytes 10076160 | tf_op jit(solution)/shard_map/all_gather | solution.py:175
  7.9 206.4 %all-gather.7.cloned.1.call-start = ((), (), s32[]{:S(2)}) async-start(), calls=%async_computation.1 | async-start | bytes 10076160 | tf_op jit(solution)/shard_map/all_gather | solution.py:176
  15.6 13.4 %collective-permute-start.4 = (f32[16,2,2,32]{3,2,1,0:T(2,128)S(1)}, f32[16,2,2,32]{3,2,1,0:T(2,128)S(1)}, u32[]{:S(2)}, u32[]{:S(2)}) collective-permute-start(f32[16,2,2,32]{3,2,1,0:T(2,128)S(1)} %add.456), channel_id=1, source_target_pairs={{0,16},{4,20},{8,24},{12,28},{16,0},{20,4},{24,8},{28,12},{32,48},... | collective-permute-start | bytes 24584 | tf_op jit(solution)/shard_map/ppermute | solution.py:25
  19.6 19.1 %collective-permute-start = (f32[2,2,1,8,192]{4,3,2,1,0:T(8,128)S(1)}, f32[2,2,1,8,192]{4,3,2,1,0:T(8,128)S(1)}, u32[]{:S(2)}, u32[]{:S(2)}) collective-permute-start(f32[2,2,1,8,192]{4,3,2,1,0:T(8,128)S(1)} %get-tuple-element.602), channel_id=1, source_target_pairs={{0,4},{4,8},{8,12},{12,16},{16,20},{20,24},{24,28},{28,32},{32,36}... | collective-permute-start | bytes 73736 | tf_op jit(solution)/shard_map/ppermute | solution.py:41
  20.9 17.8 %collective-permute-start.1 = (f32[2,2,1,8,192]{4,3,2,1,0:T(8,128)S(1)}, f32[2,2,1,8,192]{4,3,2,1,0:T(8,128)S(1)}, u32[]{:S(2)}, u32[]{:S(2)}) collective-permute-start(f32[2,2,1,8,192]{4,3,2,1,0:T(8,128)S(1)} %get-tuple-element.603), channel_id=1, source_target_pairs={{4,0},{8,4},{12,8},{16,12},{20,16},{24,20},{28,24},{32,28},{36,32}... | collective-permute-start | bytes 73736 | tf_op jit(solution)/shard_map/ppermute | solution.py:42
  22.2 804.2 %all-reduce.21.cloned.1.call-start = ((), (), s32[]{:S(2)}) async-start(), calls=%async_computation.2 | async-start | bytes 7995392 | tf_op jit(solution)/shard_map/psum | solution.py:158
  29.1 9.1 collective-permute-start.5
  102.7 5.5 collective-permute-start.10
  111.4 4.8 collective-permute-start.7
  129.3 5.5 collective-permute-start.16
  136.9 4.6 collective-permute-start.13
  156.2 5.9 collective-permute-start.22
  176.1 16.1 %collective-permute-start.26 = (f32[16,2,2,32]{3,2,1,0:T(2,128)S(1)}, f32[16,2,2,32]{3,2,1,0:T(2,128)S(1)}, u32[]{:S(2)}, u32[]{:S(2)}) collective-permute-start(f32[16,2,2,32]{3,2,1,0:T(2,128)S(1)} %constant_dynamic-update-slice_fusion.7), channel_id=1, source_target_pairs={{0,4},{4,0},{8,12},{12,8},{16,20},{20,16},{24,28},{28,24},{32,36},... | collective-permute-start | bytes 24584 | tf_op jit(solution)/shard_map/ppermute | solution.py:25
  179.8 19.4 %collective-permute-start.49 = (bf16[2,2,1,8,192]{4,3,2,1,0:T(8,128)(2,1)S(1)}, bf16[2,2,1,8,192]{4,3,2,1,0:T(8,128)(2,1)S(1)}, u32[]{:S(2)}, u32[]{:S(2)}) collective-permute-start(bf16[2,2,1,8,192]{4,3,2,1,0:T(8,128)(2,1)S(1)} %get-tuple-element.587), channel_id=1, source_target_pairs={{4,0},{8,4},{12,8},{16,12},{20,16},{24,20},{28,24},{32,28},{36,32}... | collective-permute-start | bytes 36872 | tf_op jit(solution)/shard_map/ppermute | solution.py:42
  181.1 39.0 %collective-permute-start.48 = (bf16[2,2,1,8,192]{4,3,2,1,0:T(8,128)(2,1)}, bf16[2,2,1,8,192]{4,3,2,1,0:T(8,128)(2,1)}, u32[]{:S(2)}, u32[]{:S(2)}) collective-permute-start(bf16[2,2,1,8,192]{4,3,2,1,0:T(8,128)(2,1)} %get-tuple-element.586), channel_id=1, source_target_pairs={{0,4},{4,8},{8,12},{12,16},{16,20},{20,24},{24,28},{28,32},{32,36}... | collective-permute-start | bytes 36872 | tf_op jit(solution)/shard_map/ppermute | solution.py:41
  196.2 5.5 collective-permute-start.28
  201.7 6.7 collective-permute-start.29
  224.9 6.2 collective-permute-start.34
  245.0 5.6 collective-permute-start.38
  250.6 8.2 collective-permute-start.39
  259.4 11.5 %collective-permute-start.40 = (f32[16,2,2,32]{3,2,1,0:T(2,128)}, f32[16,2,2,32]{3,2,1,0:T(2,128)}, u32[]{:S(2)}, u32[]{:S(2)}) collective-permute-start(f32[16,2,2,32]{3,2,1,0:T(2,128)} %add.507), channel_id=1, source_target_pairs={{0,16},{4,20},{8,24},{12,28},{16,0},{20,4},{24,8},{28,12},{32,48},... | collective-permute-start | bytes 24584 | tf_op jit(solution)/shard_map/ppermute | solution.py:25
  272.5 8.7 collective-permute-start.36
  274.4 6.7 collective-permute-start.37
  304.8 7.1 collective-permute-start.44
  313.2 7.3 collective-permute-start.45
  321.9 9.6 collective-permute-start.46
  332.9 10.4 collective-permute-start.47
  361.9 10.1 collective-permute-start.52
  377.0 8.2 collective-permute-start.54
  381.7 15.0 %collective-permute-start.42 = (f32[2,2,1,8,192]{4,3,2,1,0:T(8,128)}, f32[2,2,1,8,192]{4,3,2,1,0:T(8,128)}, u32[]{:S(2)}, u32[]{:S(2)}) collective-permute-start(f32[2,2,1,8,192]{4,3,2,1,0:T(8,128)} %get-tuple-element.96), channel_id=1, source_target_pairs={{0,4},{4,8},{8,12},{12,16},{16,20},{20,24},{24,28},{28,32},{32,36}... | collective-permute-start | bytes 73736 | tf_op jit(solution)/shard_map/ppermute | solution.py:41
  383.9 12.8 %collective-permute-start.43 = (f32[2,2,1,8,192]{4,3,2,1,0:T(8,128)}, f32[2,2,1,8,192]{4,3,2,1,0:T(8,128)}, u32[]{:S(2)}, u32[]{:S(2)}) collective-permute-start(f32[2,2,1,8,192]{4,3,2,1,0:T(8,128)} %get-tuple-element.97), channel_id=1, source_target_pairs={{4,0},{8,4},{12,8},{16,12},{20,16},{24,20},{28,24},{32,28},{36,32}... | collective-permute-start | bytes 73736 | tf_op jit(solution)/shard_map/ppermute | solution.py:42
  385.2 8.5 collective-permute-start.55
  415.8 7.9 collective-permute-start.58
  425.0 10.9 %collective-permute-start.59 = (f32[2,2,32]{2,1,0:T(2,128)}, f32[2,2,32]{2,1,0:T(2,128)}, u32[]{:S(2)}, u32[]{:S(2)}) collective-permute-start(f32[2,2,32]{2,1,0:T(2,128)} %fusion.217), channel_id=1, source_target_pairs={{0,8},{4,12},{8,0},{12,4},{16,24},{20,28},{24,16},{28,20},{32,40},... | collective-permute-start | bytes 1544 | tf_op jit(solution)/shard_map/ppermute | solution.py:25
  436.6 7.8 collective-permute-start.60
  444.4 4.5 collective-permute-start.61
  445.9 4.5 collective-permute-start.56
  447.2 5.0 collective-permute-start.57
  471.2 25.2 %collective-permute-start.64 = (f32[2,2,32]{2,1,0:T(2,128)}, f32[2,2,32]{2,1,0:T(2,128)}, u32[]{:S(2)}, u32[]{:S(2)}) collective-permute-start(f32[2,2,32]{2,1,0:T(2,128)} %pad_maximum_fusion.43), channel_id=1, source_target_pairs={{0,4},{4,0},{8,12},{12,8},{16,20},{20,16},{24,28},{28,24},{32,36},... | collective-permute-start | bytes 1544 | tf_op jit(solution)/shard_map/ppermute | solution.py:25
  501.4 6.4 collective-permute-start.66
  510.4 4.9 collective-permute-start.63
  530.2 5.1 collective-permute-start.72
  557.8 5.1 collective-permute-start.78
  582.4 4.6 collective-permute-start.83
  587.0 5.2 collective-permute-start.84
  606.5 11.9 %collective-permute-start.88 = (f32[2,2,32]{2,1,0:T(2,128)S(1)}, f32[2,2,32]{2,1,0:T(2,128)S(1)}, u32[]{:S(2)}, u32[]{:S(2)}) collective-permute-start(f32[2,2,32]{2,1,0:T(2,128)S(1)} %pad_maximum_fusion.47), channel_id=1, source_target_pairs={{0,4},{4,0},{8,12},{12,8},{16,20},{20,16},{24,28},{28,24},{32,36},... | collective-permute-start | bytes 1544 | tf_op jit(solution)/shard_map/ppermute | solution.py:25
  622.1 8.8 collective-permute-start.90
  630.8 407.8 %all-reduce.23.cloned.1.call-start = ((), (), s32[]{:S(2)}) async-start(), calls=%async_computation.3 | async-start | bytes 7995392
  (114 other events, 2049.5 us)
Sparse Core Ops, SparseCore 0:
  9.8 84.5 all-gather.4
  96.2 83.8 all-gather.6
  631.0 195.4 all-reduce.20
  843.9 194.6 all-reduce.22
where the time goes:
time: 1060 us; the launch traced here: 1050 us
  waiting for transfers between devices  503 us (47%)
  local copies, waits for them, and re-layouts  216 us (20%)
  starting transfers between devices  189 us (18%)
  other arithmetic  61.1 us (6%)
  matrix products  49.6 us (5%)
  between operations  17.3 us (2%)
  blocking collectives  14.2 us (1%)
    unnamed x5, waiting for transfers between devices  192 us
    psum x1, waiting for transfers between devices, reduced_grads(): lax.psum(packed, ('rows', 'dp'))  182 us
    ppermute x60, starting transfers between devices, rows_allsum(): value = value + lax.ppermute(value, 'rows', partner)  142 us
    all_gather x1, waiting for transfers between devices, on_device(): enc_all = lax.all_gather(enc_weight[0], 'section')  53.7 us
    ppermute x60, waiting for transfers between devices, rows_allsum(): value = value + lax.ppermute(value, 'rows', partner)  49.2 us
    transpose x16, local copies, waits for them, and re-layouts, flipped(): return jnp.swapaxes(blocks, 1, 2).reshape(-1, blocks.shape[1])  48.1 us
    dot_general x15, matrix products, conv_rows(): out = jnp.dot(patches, weights, preferred_element_type=jnp.float32)  43.2 us
    concatenate x17, local copies, waits for them, and re-layouts, gather_patches(): jnp.concatenate(pieces, axis=-1)  43 us
  transfers between devices with their start and end apart: 96, of which 47 were waited for; matrix products, arithmetic and copies ran while one was open for 17% of the time, Pallas kernels for 0%

commit v1 on v0

--- a/solution.py
+++ b/solution.py
@@ -144,22 +144,44 @@
     )
 
 
-def reduced_grads(weight_grad, gain_grad, form, after=None):
+def halving_order(bits):
+    order = [b for b in (0, 1, bits - 1) if 0 <= b < bits]
+    order = list(dict.fromkeys(order))
+    return order + [b for b in range(bits) if b not in order]
+
+
+def tree_scatter(packed):
+    row_count = lax.axis_size("rows")
+    dp_count = lax.axis_size("dp")
+    if (row_count & (row_count - 1)) or (dp_count & (dp_count - 1)):
+        return lax.psum_scatter(packed, ("rows", "dp"), scatter_dimension=0, tiled=True)[0]
+    row_bits = row_count.bit_length() - 1
+    dp_bits = dp_count.bit_length() - 1
+    names = [("rows", row_bits - 1 - k) for k in range(row_bits)]
+    names += [("dp", dp_bits - 1 - k) for k in range(dp_bits)]
+    buf = packed.reshape((2,) * (row_bits + dp_bits) + packed.shape[1:])
+    steps = [("rows", b) for b in halving_order(row_bits)] + [("dp", b) for b in range(dp_bits)]
+    for axis, bit in steps:
+        place = names.index((axis, bit))
+        mine = (lax.axis_index(axis) >> bit) & 1
+        keep = lax.dynamic_index_in_dim(buf, mine, place, keepdims=False)
+        send = lax.dynamic_index_in_dim(buf, 1 - mine, place, keepdims=False)
+        count = lax.axis_size(axis)
+        buf = keep + lax.ppermute(send, axis, [(i, i ^ (1 << bit)) for i in range(count)])
+        names.pop(place)
+    return buf
+
+
+def reduced_grads(weight_grad, gain_grad):
     shards = lax.axis_size("rows") * lax.axis_size("dp")
     rows_out = weight_grad.shape[0] // shards
     gains_out = gain_grad.shape[0] // shards
-    position = lax.axis_index("rows") * lax.axis_size("dp") + lax.axis_index("dp")
     packed = jnp.concatenate(
         [weight_grad.reshape(shards, -1), gain_grad.reshape(shards, gains_out)], axis=1
     )
-    if after is not None:
-        packed = packed + 0.0 * after[:1, :1]
-    if form == "sum":
-        total = lax.dynamic_index_in_dim(lax.psum(packed, ("rows", "dp")), position, 0, keepdims=False)
-    else:
-        total = lax.psum_scatter(packed, ("rows", "dp"), scatter_dimension=0, tiled=True)[0]
+    total = tree_scatter(packed)
     split = rows_out * weight_grad.shape[1]
-    return total[:split].reshape(rows_out, weight_grad.shape[1]), total[split:], packed[0, 0]
+    return total[:split].reshape(rows_out, weight_grad.shape[1]), total[split:]
 
 
 def on_device(latent, enc_weight, dec_weight, enc_gain, dec_gain, out_grad):
@@ -228,7 +250,7 @@
         lax.dynamic_index_in_dim(jnp.stack(dec_cots), section_pos, 0, keepdims=False),
     )
     dec_gain_own = lax.dynamic_index_in_dim(jnp.stack(dec_gain_parts), section_pos, 0, keepdims=False)
-    dec_result, dec_gains_out, _ = reduced_grads(own_dec, dec_gain_own, "sum")
+    dec_result, dec_gains_out = reduced_grads(own_dec, dec_gain_own)
 
     enc_cots = [None] * levels
     enc_gain_parts = [None] * levels
@@ -247,13 +269,12 @@
       cot = passed + skip_grads[level]
       enc_cots[level] = cot_low
       enc_gain_parts[level] = gain_part
-    late_pos = section_pos + (0.0 * dec_result[0, 0]).astype(section_pos.dtype)
     own_enc = weight_gradient(
-        lax.dynamic_index_in_dim(jnp.stack(enc_active), late_pos, 0, keepdims=False),
-        lax.dynamic_index_in_dim(jnp.stack(enc_cots), late_pos, 0, keepdims=False),
-    )
-    enc_gain_own = lax.dynamic_index_in_dim(jnp.stack(enc_gain_parts), late_pos, 0, keepdims=False)
-    enc_result, enc_gains_out, _ = reduced_grads(own_enc, enc_gain_own, "scatter", dec_result)
+        lax.dynamic_index_in_dim(jnp.stack(enc_active), section_pos, 0, keepdims=False),
+        lax.dynamic_index_in_dim(jnp.stack(enc_cots), section_pos, 0, keepdims=False),
+    )
+    enc_gain_own = lax.dynamic_index_in_dim(jnp.stack(enc_gain_parts), section_pos, 0, keepdims=False)
+    enc_result, enc_gains_out = reduced_grads(own_enc, enc_gain_own)
     return (enc_result[None], dec_result[None], enc_gains_out[None], dec_gains_out[None])
 
 

time: 1060 us -> 769 us (0.73)
  the two profiles are of different devices: /device:TPU:6 before, /device:TPU:16 now
where the time goes in v1:
time: 769 us; the launch traced here: 755 us
  local copies, waits for them, and re-layouts  214 us (28%)
  starting transfers between devices  198 us (26%)
  waiting for transfers between devices  198 us (26%)
  other arithmetic  61.4 us (8%)
  matrix products  48.1 us (6%)
  between operations  17.4 us (2%)
  blocking collectives  16.7 us (2%)
    ppermute x60, starting transfers between devices, rows_allsum(): value = value + lax.ppermute(value, 'rows', partner)  80.6 us
    ppermute x60, waiting for transfers between devices, rows_allsum(): value = value + lax.ppermute(value, 'rows', partner)  72 us
    all_gather x1, waiting for transfers between devices, on_device(): enc_all = lax.all_gather(enc_weight[0], 'section')  59.2 us
    ppermute x16, starting transfers between devices, edge_rows(): high = lax.ppermute(block[:, :, :1], 'rows', down)  57.9 us
    ppermute x12, waiting for transfers between devices, tree_scatter(): lax.ppermute(send, axis, [(i, i ^ 1 << bit) for i in range(count)])  55.4 us
    transpose x16, local copies, waits for them, and re-layouts, flipped(): return jnp.swapaxes(blocks, 1, 2).reshape(-1, blocks.shape[1])  48 us
    concatenate x17, local copies, waits for them, and re-layouts, gather_patches(): jnp.concatenate(pieces, axis=-1)  41.8 us
    dot_general x15, matrix products, conv_rows(): out = jnp.dot(patches, weights, preferred_element_type=jnp.float32)  41.7 us
  transfers between devices with their start and end apart: 106, of which 49 were waited for; matrix products, arithmetic and copies ran while one was open for 25% of the time, Pallas kernels for 0%

profile of v1, /device:TPU:16, one launch (start us, length us, event | category | flops | bytes accessed | tf_op | source)
XLA Modules:
  0.0 754.8 jit_solution(14402928366532872517)
XLA Ops:
  21.7 8.0 %all-gather = f32[4,1,192]{2,1,0:T(1,128)S(1)} all-gather(f32[1,1,192]{2,1,0:T(1,128)S(1)} %bitcast.566), channel_id=1, replica_groups=mesh['section'=4,'rows'=16,'dp'=4] {'section'}, dimensions={0}, use_global_device_ids=true | all-gather | bytes 3840 | tf_op jit(solution)/shard_map/all_gather | solution.py:199
  36.3 59.2 %all-gather.5.cloned.1.call-done = bf16[4,5184,192]{1,2,0:T(8,128)(2,1)} async-done(((bf16[1,5184,192]{1,2,0:T(8,128)(2,1)}), bf16[4,5184,192]{1,2,0:T(8,128)(2,1)}) %all-gather.5.cloned.1.call-update) | async-done | bytes 7962640 | tf_op jit(solution)/shard_map/all_gather | solution.py:197
  104.4 4.9 collective-permute-done.10
  130.7 4.8 collective-permute-done.16
  137.8 3.8 collective-permute-start.13
  156.3 5.4 collective-permute-done.22
  186.7 8.7 %all-gather.1 = f32[4,1,192]{2,1,0:T(1,128)S(1)} all-gather(f32[1,1,192]{2,1,0:T(1,128)S(1)} %bitcast.567), channel_id=1, replica_groups=mesh['section'=4,'rows'=16,'dp'=4] {'section'}, dimensions={0}, use_global_device_ids=true | all-gather | bytes 3840 | tf_op jit(solution)/shard_map/all_gather | solution.py:200
  196.5 4.4 collective-permute-done.30
  224.0 5.4 collective-permute-done.36
  231.5 3.9 collective-permute-start.33
  252.6 5.8 fusion.246
  276.5 5.7 fusion.245
  282.2 3.9 copy.99
  287.3 5.9 collective-permute-start.45
  294.9 3.8 copy.47
  302.0 3.8 copy.50
  309.1 4.5 copy.45
  313.6 3.8 copy.53
  324.5 4.0 multiply_reduce_fusion.3
  337.4 4.5 copy.48
  342.0 3.8 copy.56
  385.1 3.9 multiply_reduce_fusion.2
  397.7 3.8 copy.59
  405.8 4.5 copy.51
  410.3 3.8 copy.62
  423.5 4.0 collective-permute-start.55
  437.8 3.9 multiply_reduce_fusion.1
  452.2 3.8 copy.66
  457.3 3.8 collective-permute-start.63
  462.8 4.7 copy.54
  470.9 4.7 copy.60
  479.0 4.6 copy.67
  484.9 4.4 collective-permute-done.64
  499.0 3.8 concatenate.296
  507.6 4.5 collective-permute-start.69
  513.8 5.0 collective-permute-done.70
  543.2 4.8 collective-permute-done.76
  551.4 3.9 collective-permute-start.73
  571.3 3.9 collective-permute-done.82
  586.6 3.8 concatenate.311
  608.8 4.0 collective-permute-start.85
  624.1 7.4 concatenate.323
  642.7 7.4 concatenate.316
  661.9 21.0 %collective-permute-done.99 = f32[2,2,2,2,15555]{4,3,2,1,0:T(2,128)S(1)} collective-permute-done((f32[2,2,2,2,15555]{4,3,2,1,0:T(2,128)S(1)}, f32[2,2,2,2,15555]{4,3,2,1,0:T(2,128)S(1)}, u32[]{:S(2)}, u32[]{:S(2)}) %collective-permute-start.99) | collective-permute-done | bytes 995552 | tf_op jit(solution)/shard_map/ppermute | solution.py:170
  684.4 19.6 %collective-permute-done.91 = f32[2,2,2,2,15555]{4,3,2,1,0:T(2,128)S(1)} collective-permute-done((f32[2,2,2,2,15555]{4,3,2,1,0:T(2,128)S(1)}, f32[2,2,2,2,15555]{4,3,2,1,0:T(2,128)S(1)}, u32[]{:S(2)}, u32[]{:S(2)}) %collective-permute-start.91) | collective-permute-done | bytes 995552 | tf_op jit(solution)/shard_map/ppermute | solution.py:170
  708.4 9.2 %collective-permute-done.92 = f32[2,2,2,15555]{3,2,1,0:T(2,128)S(1)} collective-permute-done((f32[2,2,2,15555]{3,2,1,0:T(2,128)S(1)}, f32[2,2,2,15555]{3,2,1,0:T(2,128)S(1)}, u32[]{:S(2)}, u32[]{:S(2)}) %collective-permute-start.92) | collective-permute-done | bytes 497792 | tf_op jit(solution)/shard_map/ppermute | solution.py:170
  722.1 4.3 collective-permute-done.93
  734.5 9.7 %collective-permute-start.95 = (f32[15555]{0:T(1024)S(1)}, f32[15555]{0:T(1024)S(1)}, u32[]{:S(2)}, u32[]{:S(2)}) collective-permute-start(f32[15555]{0:T(1024)S(1)} %get-tuple-element.27), channel_id=1, source_target_pairs={{0,2},{1,3},{2,0},{3,1},{4,6},{5,7},{6,4},{7,5},{8,10},{9,11},{10,... | collective-permute-start | bytes 186668 | tf_op jit(solution)/shard_map/ppermute | solution.py:170
  (845 shorter events, 416.8 us)
Async XLA Ops:
  7.2 88.3 %all-gather.5.cloned.1.call-start = ((), (), s32[]{:S(2)}) async-start(), calls=%async_computation | async-start | bytes 10076160 | tf_op jit(solution)/shard_map/all_gather | solution.py:197
  7.9 204.2 %all-gather.7.cloned.1.call-start = ((), (), s32[]{:S(2)}) async-start(), calls=%async_computation.1 | async-start | bytes 10076160 | tf_op jit(solution)/shard_map/all_gather | solution.py:198
  14.0 15.8 %collective-permute-start.4 = (f32[16,2,2,32]{3,2,1,0:T(2,128)S(1)}, f32[16,2,2,32]{3,2,1,0:T(2,128)S(1)}, u32[]{:S(2)}, u32[]{:S(2)}) collective-permute-start(f32[16,2,2,32]{3,2,1,0:T(2,128)S(1)} %add.526), channel_id=1, source_target_pairs={{0,16},{4,20},{8,24},{12,28},{16,0},{20,4},{24,8},{28,12},{32,48},... | collective-permute-start | bytes 24584 | tf_op jit(solution)/shard_map/ppermute | solution.py:25
  16.1 18.2 %collective-permute-start = (f32[2,2,1,8,192]{4,3,2,1,0:T(8,128)S(1)}, f32[2,2,1,8,192]{4,3,2,1,0:T(8,128)S(1)}, u32[]{:S(2)}, u32[]{:S(2)}) collective-permute-start(f32[2,2,1,8,192]{4,3,2,1,0:T(8,128)S(1)} %get-tuple-element.598), channel_id=1, source_target_pairs={{0,4},{4,8},{8,12},{12,16},{16,20},{20,24},{24,28},{28,32},{32,36}... | collective-permute-start | bytes 73736 | tf_op jit(solution)/shard_map/ppermute | solution.py:41
  18.0 16.2 %collective-permute-start.1 = (f32[2,2,1,8,192]{4,3,2,1,0:T(8,128)S(1)}, f32[2,2,1,8,192]{4,3,2,1,0:T(8,128)S(1)}, u32[]{:S(2)}, u32[]{:S(2)}) collective-permute-start(f32[2,2,1,8,192]{4,3,2,1,0:T(8,128)S(1)} %get-tuple-element.599), channel_id=1, source_target_pairs={{4,0},{8,4},{12,8},{16,12},{20,16},{24,20},{28,24},{32,28},{36,32}... | collective-permute-start | bytes 73736 | tf_op jit(solution)/shard_map/ppermute | solution.py:42
  109.3 7.2 collective-permute-start.11
  135.5 6.1 collective-permute-start.17
  135.9 6.2 collective-permute-start.12
  161.8 6.6 collective-permute-start.23
  179.4 16.0 %collective-permute-start.29 = (f32[16,2,2,32]{3,2,1,0:T(2,128)S(1)}, f32[16,2,2,32]{3,2,1,0:T(2,128)S(1)}, u32[]{:S(2)}, u32[]{:S(2)}) collective-permute-start(f32[16,2,2,32]{3,2,1,0:T(2,128)S(1)} %constant_dynamic-update-slice_fusion.6), channel_id=1, source_target_pairs={{0,8},{4,12},{8,0},{12,4},{16,24},{20,28},{24,16},{28,20},{32,40},... | collective-permute-start | bytes 24584 | tf_op jit(solution)/shard_map/ppermute | solution.py:25
  182.4 35.2 %collective-permute-start.25 = (bf16[2,2,1,8,192]{4,3,2,1,0:T(8,128)(2,1)}, bf16[2,2,1,8,192]{4,3,2,1,0:T(8,128)(2,1)}, u32[]{:S(2)}, u32[]{:S(2)}) collective-permute-start(bf16[2,2,1,8,192]{4,3,2,1,0:T(8,128)(2,1)} %get-tuple-element.583), channel_id=1, source_target_pairs={{4,0},{8,4},{12,8},{16,12},{20,16},{24,20},{28,24},{32,28},{36,32}... | collective-permute-start | bytes 36872 | tf_op jit(solution)/shard_map/ppermute | solution.py:42
  184.3 37.7 %collective-permute-start.24 = (bf16[2,2,1,8,192]{4,3,2,1,0:T(8,128)(2,1)}, bf16[2,2,1,8,192]{4,3,2,1,0:T(8,128)(2,1)}, u32[]{:S(2)}, u32[]{:S(2)}) collective-permute-start(bf16[2,2,1,8,192]{4,3,2,1,0:T(8,128)(2,1)} %get-tuple-element.582), channel_id=1, source_target_pairs={{0,4},{4,8},{8,12},{12,16},{16,20},{20,24},{24,28},{28,32},{32,36}... | collective-permute-start | bytes 36872 | tf_op jit(solution)/shard_map/ppermute | solution.py:41
  229.5 6.3 collective-permute-start.32
  258.5 6.4 collective-permute-start.43
  274.7 11.3 %collective-permute-start.44 = (f32[16,2,2,32]{3,2,1,0:T(2,128)}, f32[16,2,2,32]{3,2,1,0:T(2,128)}, u32[]{:S(2)}, u32[]{:S(2)}) collective-permute-start(f32[16,2,2,32]{3,2,1,0:T(2,128)} %constant_dynamic-update-slice_fusion.1), channel_id=1, source_target_pairs={{0,4},{4,0},{8,12},{12,8},{16,20},{20,16},{24,28},{28,24},{32,36},... | collective-permute-start | bytes 24584 | tf_op jit(solution)/shard_map/ppermute | solution.py:25
  287.3 11.4 %collective-permute-start.45 = (f32[16,2,2,32]{3,2,1,0:T(2,128)}, f32[16,2,2,32]{3,2,1,0:T(2,128)}, u32[]{:S(2)}, u32[]{:S(2)}) collective-permute-start(f32[16,2,2,32]{3,2,1,0:T(2,128)} %constant_dynamic-update-slice_fusion), channel_id=1, source_target_pairs={{0,8},{4,12},{8,0},{12,4},{16,24},{20,28},{24,16},{28,20},{32,40},... | collective-permute-start | bytes 24584 | tf_op jit(solution)/shard_map/ppermute | solution.py:25
  307.3 10.1 %collective-permute-start.47 = (f32[16,2,2,32]{3,2,1,0:T(2,128)}, f32[16,2,2,32]{3,2,1,0:T(2,128)}, u32[]{:S(2)}, u32[]{:S(2)}) collective-permute-start(f32[16,2,2,32]{3,2,1,0:T(2,128)} %add.588), channel_id=1, source_target_pairs={{0,32},{4,36},{8,40},{12,44},{16,48},{20,52},{24,56},{28,60},{32,0... | collective-permute-start | bytes 24584 | tf_op jit(solution)/shard_map/ppermute | solution.py:25
  335.3 10.5 %collective-permute-start.50 = (f32[2,2,32]{2,1,0:T(2,128)}, f32[2,2,32]{2,1,0:T(2,128)}, u32[]{:S(2)}, u32[]{:S(2)}) collective-permute-start(f32[2,2,32]{2,1,0:T(2,128)} %pad_maximum_fusion.40), channel_id=1, source_target_pairs={{0,4},{4,0},{8,12},{12,8},{16,20},{20,16},{24,28},{28,24},{32,36},... | collective-permute-start | bytes 1544 | tf_op jit(solution)/shard_map/ppermute | solution.py:25
  350.8 9.6 %collective-permute-start.52 = (f32[2,2,32]{2,1,0:T(2,128)S(1)}, f32[2,2,32]{2,1,0:T(2,128)S(1)}, u32[]{:S(2)}, u32[]{:S(2)}) collective-permute-start(f32[2,2,32]{2,1,0:T(2,128)S(1)} %fusion.314), channel_id=1, source_target_pairs={{0,16},{4,20},{8,24},{12,28},{16,0},{20,4},{24,8},{28,12},{32,48},... | collective-permute-start | bytes 1544 | tf_op jit(solution)/shard_map/ppermute | solution.py:25
  354.9 22.1 %collective-permute-start.96 = (f32[2,2,1,8,192]{4,3,2,1,0:T(8,128)}, f32[2,2,1,8,192]{4,3,2,1,0:T(8,128)}, u32[]{:S(2)}, u32[]{:S(2)}) collective-permute-start(f32[2,2,1,8,192]{4,3,2,1,0:T(8,128)} %get-tuple-element.92), channel_id=1, source_target_pairs={{0,4},{4,8},{8,12},{12,16},{16,20},{20,24},{24,28},{28,32},{32,36}... | collective-permute-start | bytes 73736 | tf_op jit(solution)/shard_map/ppermute | solution.py:41
  356.8 20.2 %collective-permute-start.97 = (f32[2,2,1,8,192]{4,3,2,1,0:T(8,128)}, f32[2,2,1,8,192]{4,3,2,1,0:T(8,128)}, u32[]{:S(2)}, u32[]{:S(2)}) collective-permute-start(f32[2,2,1,8,192]{4,3,2,1,0:T(8,128)} %get-tuple-element.93), channel_id=1, source_target_pairs={{4,0},{8,4},{12,8},{16,12},{20,16},{24,20},{28,24},{32,28},{36,32}... | collective-permute-start | bytes 73736 | tf_op jit(solution)/shard_map/ppermute | solution.py:42
  360.5 9.2 %collective-permute-start.53 = (f32[2,2,32]{2,1,0:T(2,128)S(1)}, f32[2,2,32]{2,1,0:T(2,128)S(1)}, u32[]{:S(2)}, u32[]{:S(2)}) collective-permute-start(f32[2,2,32]{2,1,0:T(2,128)S(1)} %add.596), channel_id=1, source_target_pairs={{0,32},{4,36},{8,40},{12,44},{16,48},{20,52},{24,56},{28,60},{32,0... | collective-permute-start | bytes 1544 | tf_op jit(solution)/shard_map/ppermute | solution.py:25
  364.1 11.0 %collective-permute-start.48 = (f32[2,2,1,8,384]{4,3,2,1,0:T(8,128)}, f32[2,2,1,8,384]{4,3,2,1,0:T(8,128)}, u32[]{:S(2)}, u32[]{:S(2)}) collective-permute-start(f32[2,2,1,8,384]{4,3,2,1,0:T(8,128)} %get-tuple-element.72), channel_id=1, source_target_pairs={{0,4},{4,8},{8,12},{12,16},{16,20},{20,24},{24,28},{28,32},{32,36}... | collective-permute-start | bytes 147464 | tf_op jit(solution)/shard_map/ppermute | solution.py:41
  366.0 10.0 %collective-permute-start.49 = (f32[2,2,1,8,384]{4,3,2,1,0:T(8,128)}, f32[2,2,1,8,384]{4,3,2,1,0:T(8,128)}, u32[]{:S(2)}, u32[]{:S(2)}) collective-permute-start(f32[2,2,1,8,384]{4,3,2,1,0:T(8,128)} %get-tuple-element.73), channel_id=1, source_target_pairs={{4,0},{8,4},{12,8},{16,12},{20,16},{24,20},{28,24},{32,28},{36,32}... | collective-permute-start | bytes 147464 | tf_op jit(solution)/shard_map/ppermute | solution.py:42
  402.8 11.4 %collective-permute-start.57 = (f32[2,2,32]{2,1,0:T(2,128)}, f32[2,2,32]{2,1,0:T(2,128)}, u32[]{:S(2)}, u32[]{:S(2)}) collective-permute-start(f32[2,2,32]{2,1,0:T(2,128)} %fusion.227), channel_id=1, source_target_pairs={{0,8},{4,12},{8,0},{12,4},{16,24},{20,28},{24,16},{28,20},{32,40},... | collective-permute-start | bytes 1544 | tf_op jit(solution)/shard_map/ppermute | solution.py:25
  420.0 7.5 collective-permute-start.59
  421.6 7.5 collective-permute-start.54
  448.5 7.5 collective-permute-start.62
  457.3 26.3 %collective-permute-start.63 = (f32[2,2,32]{2,1,0:T(2,128)}, f32[2,2,32]{2,1,0:T(2,128)}, u32[]{:S(2)}, u32[]{:S(2)}) collective-permute-start(f32[2,2,32]{2,1,0:T(2,128)} %fusion.226), channel_id=1, source_target_pairs={{0,8},{4,12},{8,0},{12,4},{16,24},{20,28},{24,16},{28,20},{32,40},... | collective-permute-start | bytes 1544 | tf_op jit(solution)/shard_map/ppermute | solution.py:25
  518.8 6.5 collective-permute-start.71
  548.0 7.2 collective-permute-start.77
  549.4 6.2 collective-permute-start.72
  575.2 6.9 collective-permute-start.83
  606.0 6.8 collective-permute-start.89
  606.8 9.1 %collective-permute-start.84 = (f32[2,2,1,8,384]{4,3,2,1,0:T(8,128)}, f32[2,2,1,8,384]{4,3,2,1,0:T(8,128)}, u32[]{:S(2)}, u32[]{:S(2)}) collective-permute-start(f32[2,2,1,8,384]{4,3,2,1,0:T(8,128)} %get-tuple-element.60), channel_id=1, source_target_pairs={{0,4},{4,8},{8,12},{12,16},{16,20},{20,24},{24,28},{28,32},{32,36}... | collective-permute-start | bytes 147464 | tf_op jit(solution)/shard_map/ppermute | solution.py:41
  608.8 8.1 %collective-permute-start.85 = (f32[2,2,1,8,384]{4,3,2,1,0:T(8,128)}, f32[2,2,1,8,384]{4,3,2,1,0:T(8,128)}, u32[]{:S(2)}, u32[]{:S(2)}) collective-permute-start(f32[2,2,1,8,384]{4,3,2,1,0:T(8,128)} %get-tuple-element.61), channel_id=1, source_target_pairs={{4,0},{8,4},{12,8},{16,12},{20,16},{24,20},{28,24},{32,28},{36,32}... | collective-permute-start | bytes 147464 | tf_op jit(solution)/shard_map/ppermute | solution.py:42
  639.2 14.1 %collective-permute-start.98 = (f32[2,2,2,2,2,15555]{5,4,3,2,1,0:T(2,128)S(1)}, f32[2,2,2,2,2,15555]{5,4,3,2,1,0:T(2,128)}, u32[]{:S(2)}, u32[]{:S(2)}) collective-permute-start(f32[2,2,2,2,2,15555]{5,4,3,2,1,0:T(2,128)S(1)} %fusion.15), channel_id=1, source_target_pairs={{0,4},{4,0},{8,12},{12,8},{16,20},{20,16},{24,28},{28,24},{32,36},... | collective-permute-start | bytes 5973128 | tf_op jit(solution)/shard_map/ppermute | solution.py:170
  652.7 7.2 collective-permute-start.90
  656.6 26.3 %collective-permute-start.99 = (f32[2,2,2,2,15555]{4,3,2,1,0:T(2,128)S(1)}, f32[2,2,2,2,15555]{4,3,2,1,0:T(2,128)S(1)}, u32[]{:S(2)}, u32[]{:S(2)}) collective-permute-start(f32[2,2,2,2,15555]{4,3,2,1,0:T(2,128)S(1)} %dynamic-slice_bitcast_fusion), channel_id=1, source_target_pairs={{0,8},{4,12},{8,0},{12,4},{16,24},{20,28},{24,16},{28,20},{32,40},... | collective-permute-start | bytes 2986568 | tf_op jit(solution)/shard_map/ppermute | solution.py:170
  661.4 42.6 %collective-permute-start.91 = (f32[2,2,2,2,15555]{4,3,2,1,0:T(2,128)S(1)}, f32[2,2,2,2,15555]{4,3,2,1,0:T(2,128)S(1)}, u32[]{:S(2)}, u32[]{:S(2)}) collective-permute-start(f32[2,2,2,2,15555]{4,3,2,1,0:T(2,128)S(1)} %dynamic-slice_bitcast_fusion.1), channel_id=1, source_target_pairs={{0,8},{4,12},{8,0},{12,4},{16,24},{20,28},{24,16},{28,20},{32,40},... | collective-permute-start | bytes 2986568 | tf_op jit(solution)/shard_map/ppermute | solution.py:170
  683.4 21.3 %collective-permute-start.100 = (f32[2,2,2,15555]{3,2,1,0:T(2,128)S(1)}, f32[2,2,2,15555]{3,2,1,0:T(2,128)S(1)}, u32[]{:S(2)}, u32[]{:S(2)}) collective-permute-start(f32[2,2,2,15555]{3,2,1,0:T(2,128)S(1)} %dynamic-slice_bitcast_fusion.2), channel_id=1, source_target_pairs={{0,32},{4,36},{8,40},{12,44},{16,48},{20,52},{24,56},{28,60},{32,0... | collective-permute-start | bytes 1493288 | tf_op jit(solution)/shard_map/ppermute | solution.py:170
  704.5 13.2 %collective-permute-start.92 = (f32[2,2,2,15555]{3,2,1,0:T(2,128)S(1)}, f32[2,2,2,15555]{3,2,1,0:T(2,128)S(1)}, u32[]{:S(2)}, u32[]{:S(2)}) collective-permute-start(f32[2,2,2,15555]{3,2,1,0:T(2,128)S(1)} %dynamic-slice_bitcast_fusion.3), channel_id=1, source_target_pairs={{0,32},{4,36},{8,40},{12,44},{16,48},{20,52},{24,56},{28,60},{32,0... | collective-permute-start | bytes 1493288 | tf_op jit(solution)/shard_map/ppermute | solution.py:170
  705.0 14.0 %collective-permute-start.101 = (f32[2,2,15555]{2,1,0:T(2,128)S(1)}, f32[2,2,15555]{2,1,0:T(2,128)S(1)}, u32[]{:S(2)}, u32[]{:S(2)}) collective-permute-start(f32[2,2,15555]{2,1,0:T(2,128)S(1)} %dynamic-slice_bitcast_fusion.4), channel_id=1, source_target_pairs={{0,16},{4,20},{8,24},{12,28},{16,0},{20,4},{24,8},{28,12},{32,48},... | collective-permute-start | bytes 746648 | tf_op jit(solution)/shard_map/ppermute | solution.py:170
  718.0 8.4 %collective-permute-start.93 = (f32[2,2,15555]{2,1,0:T(2,128)S(1)}, f32[2,2,15555]{2,1,0:T(2,128)S(1)}, u32[]{:S(2)}, u32[]{:S(2)}) collective-permute-start(f32[2,2,15555]{2,1,0:T(2,128)S(1)} %dynamic-slice_bitcast_fusion.5), channel_id=1, source_target_pairs={{0,16},{4,20},{8,24},{12,28},{16,0},{20,4},{24,8},{28,12},{32,48},... | collective-permute-start | bytes 746648 | tf_op jit(solution)/shard_map/ppermute | solution.py:170
  719.5 10.0 %collective-permute-start.102 = (f32[2,15555]{1,0:T(2,128)S(1)}, f32[2,15555]{1,0:T(2,128)S(1)}, u32[]{:S(2)}, u32[]{:S(2)}) collective-permute-start(f32[2,15555]{1,0:T(2,128)S(1)} %bitcast.474), channel_id=1, source_target_pairs={{0,1},{1,0},{2,3},{3,2},{4,5},{5,4},{6,7},{7,6},{8,9},{9,8},{10,11... | collective-permute-start | bytes 373328 | tf_op jit(solution)/shard_map/ppermute | solution.py:170
  726.8 7.2 collective-permute-start.94
  729.9 14.2 %collective-permute-start.103 = (f32[15555]{0:T(1024)S(1)}, f32[15555]{0:T(1024)S(1)}, u32[]{:S(2)}, u32[]{:S(2)}) collective-permute-start(f32[15555]{0:T(1024)S(1)} %get-tuple-element.25), channel_id=1, source_target_pairs={{0,2},{1,3},{2,0},{3,1},{4,6},{5,7},{6,4},{7,5},{8,10},{9,11},{10,... | collective-permute-start | bytes 186668 | tf_op jit(solution)/shard_map/ppermute | solution.py:170
  734.5 11.9 %collective-permute-start.95 = (f32[15555]{0:T(1024)S(1)}, f32[15555]{0:T(1024)S(1)}, u32[]{:S(2)}, u32[]{:S(2)}) collective-permute-start(f32[15555]{0:T(1024)S(1)} %get-tuple-element.27), channel_id=1, source_target_pairs={{0,2},{1,3},{2,0},{3,1},{4,6},{5,7},{6,4},{7,5},{8,10},{9,11},{10,... | collective-permute-start | bytes 186668 | tf_op jit(solution)/shard_map/ppermute | solution.py:170
  (139 other events, 1242.2 us)
Sparse Core Ops, SparseCore 0:
  9.8 85.6 all-gather.4
  97.3 83.8 all-gather.6

commit v2 on v1

--- a/solution.py
+++ b/solution.py
@@ -184,6 +184,32 @@
     return total[:split].reshape(rows_out, weight_grad.shape[1]), total[split:]
 
 
+def section_gather(value):
+    count = lax.axis_size("section")
+    if count & (count - 1):
+        return lax.all_gather(value, "section")
+    slots = jnp.zeros((count,) + value.shape, value.dtype)
+    slots = lax.dynamic_update_index_in_dim(slots, value, lax.axis_index("section"), 0)
+    mask = 1
+    while mask < count:
+        slots = slots + lax.ppermute(slots, "section", [(i, i ^ mask) for i in range(count)])
+        mask *= 2
+    return slots
+
+
+def section_weights(weights):
+    rows_count = lax.axis_size("rows")
+    half = weights.shape[0] // 2
+    if rows_count % 2 or weights.shape[0] % 2:
+        return lax.all_gather(weights, "section")
+    core = lax.axis_index("rows") % 2
+    mine = lax.all_gather(lax.dynamic_slice_in_dim(weights, core * half, half, 0), "section")
+    other = lax.ppermute(mine, "rows", [(i, i ^ 1) for i in range(rows_count)])
+    low = jnp.where(core == 0, mine, other)
+    high = jnp.where(core == 0, other, mine)
+    return jnp.concatenate([low, high], axis=1)
+
+
 def on_device(latent, enc_weight, dec_weight, enc_gain, dec_gain, out_grad):
     section_pos = lax.axis_index("section")
     rows_pos = lax.axis_index("rows")
@@ -194,10 +220,11 @@
     counted = frames * rows_here * columns * (channels // GROUPS) * lax.axis_size("rows")
     cells_all = batches * lax.axis_size("dp") * frames * rows_here * lax.axis_size("rows") * columns
     loss_scale = 1.0 / math.sqrt(cells_all)
-    enc_all = lax.all_gather(enc_weight[0], "section")
-    dec_all = lax.all_gather(dec_weight[0], "section")
-    enc_gains = lax.all_gather(enc_gain[0], "section")
-    dec_gains = lax.all_gather(dec_gain[0], "section")
+    enc_all = section_weights(enc_weight[0])
+    dec_all = section_weights(dec_weight[0])
+    gains_all = section_gather(jnp.stack([enc_gain[0], dec_gain[0]]))
+    enc_gains = gains_all[:, 0]
+    dec_gains = gains_all[:, 1]
 
     hidden = latent.astype(jnp.float32)
     enc_inputs = []

time: 769 us -> 754 us (0.980)
  the two profiles are of different devices: /device:TPU:16 before, /device:TPU:8 now
where the time goes in v2:
time: 754 us; the launch traced here: 740 us
  starting transfers between devices  228 us (30%)
  local copies, waits for them, and re-layouts  215 us (29%)
  waiting for transfers between devices  177 us (23%)
  other arithmetic  53.5 us (7%)
  matrix products  48.6 us (6%)
  between operations  17.6 us (2%)
    ppermute x60, starting transfers between devices, rows_allsum(): value = value + lax.ppermute(value, 'rows', partner)  104 us
    transpose x16, local copies, waits for them, and re-layouts, flipped(): return jnp.swapaxes(blocks, 1, 2).reshape(-1, blocks.shape[1])  64.9 us
    ppermute x16, starting transfers between devices, edge_rows(): high = lax.ppermute(block[:, :, :1], 'rows', down)  55.1 us
    ppermute x12, waiting for transfers between devices, tree_scatter(): lax.ppermute(send, axis, [(i, i ^ 1 << bit) for i in range(count)])  54.7 us
    all_gather x2, waiting for transfers between devices, section_weights(): lax.all_gather(lax.dynamic_slice_in_dim(weights, core * half, half, 0), '...  53.2 us
    ppermute x60, waiting for transfers between devices, rows_allsum(): value = value + lax.ppermute(value, 'rows', partner)  53 us
    concatenate x17, local copies, waits for them, and re-layouts, gather_patches(): jnp.concatenate(pieces, axis=-1)  52.3 us
    dot_general x15, matrix products, conv_rows(): out = jnp.dot(patches, weights, preferred_element_type=jnp.float32)  42.2 us
  transfers between devices with their start and end apart: 110, of which 51 were waited for; matrix products, arithmetic and copies ran while one was open for 28% of the time, Pallas kernels for 0%

profile of v2, /device:TPU:8, one launch (start us, length us, event | category | flops | bytes accessed | tf_op | source)
XLA Modules:
  0.0 739.7 jit_solution(12640692824541825614)
XLA Ops:
  10.2 53.2 %all-gather.3.cloned.1.call-done = bf16[4,2592,192]{1,2,0:T(8,128)(2,1)} async-done(((bf16[1,2592,192]{1,2,0:T(8,128)(2,1)}), bf16[4,2592,192]{1,2,0:T(8,128)(2,1)}) %all-gather.3.cloned.1.call-update) | async-done | bytes 3981328 | tf_op jit(solution)/shard_map/all_gather | solution.py:206
  88.6 4.1 broadcast_select_fusion.2
  92.7 5.0 pad_maximum_fusion.1
  106.5 3.9 collective-permute-done.13
  130.0 3.9 collective-permute-done.18
  134.8 4.6 collective-permute-done.19
  162.5 5.5 collective-permute-start.25
  189.3 3.8 broadcast_select_fusion
  193.2 4.4 collective-permute-start.33
  197.6 5.3 pad_maximum_fusion
  228.8 5.4 collective-permute-start.40
  236.1 3.9 collective-permute-start.41
  249.0 3.6 concatenate.283
  261.4 5.5 collective-permute-start.46
  280.2 3.7 concatenate.288
  292.1 3.7 concatenate.289
  295.8 4.3 copy.44
  303.9 4.3 copy.47
  308.2 4.1 collective-permute-start.50
  315.9 4.3 copy.50
  325.2 4.3 copy.53
  329.6 4.6 copy.45
  342.0 4.3 copy.56
  346.4 4.6 copy.48
  358.6 3.6 collective-permute-start.101
  375.5 3.7 concatenate.294
  389.4 4.3 copy.59
  397.6 4.3 copy.62
  401.8 4.5 copy.51
  406.4 4.4 collective-permute-start.62
  423.6 3.6 concatenate.299
  444.0 4.5 copy.54
  448.6 4.6 copy.57
  453.1 4.5 copy.60
  457.6 4.5 copy.63
  462.2 4.5 copy.67
  466.7 4.3 collective-permute-start.68
  496.3 4.2 collective-permute-start.74
  505.5 3.9 collective-permute-start.71
  524.0 4.2 collective-permute-start.80
  604.3 7.3 concatenate.331
  616.8 3.8 fusion.21
  626.2 7.3 concatenate.324
  643.4 21.4 %collective-permute-done.103 = f32[2,2,2,2,15555]{4,3,2,1,0:T(2,128)S(1)} collective-permute-done((f32[2,2,2,2,15555]{4,3,2,1,0:T(2,128)S(1)}, f32[2,2,2,2,15555]{4,3,2,1,0:T(2,128)S(1)}, u32[]{:S(2)}, u32[]{:S(2)}) %collective-permute-start.103) | collective-permute-done | bytes 995552 | tf_op jit(solution)/shard_map/ppermute | solution.py:170
  667.3 18.2 %collective-permute-done.95 = f32[2,2,2,2,15555]{4,3,2,1,0:T(2,128)S(1)} collective-permute-done((f32[2,2,2,2,15555]{4,3,2,1,0:T(2,128)S(1)}, f32[2,2,2,2,15555]{4,3,2,1,0:T(2,128)S(1)}, u32[]{:S(2)}, u32[]{:S(2)}) %collective-permute-start.95) | collective-permute-done | bytes 995552 | tf_op jit(solution)/shard_map/ppermute | solution.py:170
  691.6 7.6 %collective-permute-done.96 = f32[2,2,2,15555]{3,2,1,0:T(2,128)S(1)} collective-permute-done((f32[2,2,2,15555]{3,2,1,0:T(2,128)S(1)}, f32[2,2,2,15555]{3,2,1,0:T(2,128)S(1)}, u32[]{:S(2)}, u32[]{:S(2)}) %collective-permute-start.96) | collective-permute-done | bytes 497792 | tf_op jit(solution)/shard_map/ppermute | solution.py:170
  699.5 4.8 collective-permute-start.97
  714.7 7.9 %collective-permute-start.107 = (f32[15555]{0:T(1024)S(1)}, f32[15555]{0:T(1024)S(1)}, u32[]{:S(2)}, u32[]{:S(2)}) collective-permute-start(f32[15555]{0:T(1024)S(1)} %get-tuple-element.25), channel_id=1, source_target_pairs={{0,2},{1,3},{2,0},{3,1},{4,6},{5,7},{6,4},{7,5},{8,10},{9,11},{10,... | collective-permute-start | bytes 186668 | tf_op jit(solution)/shard_map/ppermute | solution.py:170
  (902 shorter events, 421.8 us)
Async XLA Ops:
  7.2 56.2 %all-gather.3.cloned.1.call-start = ((), (), s32[]{:S(2)}) async-start(), calls=%async_computation | async-start | bytes 5160960 | tf_op jit(solution)/shard_map/all_gather | solution.py:206
  10.2 124.7 %all-gather.5.cloned.1.call-start = ((), (), s32[]{:S(2)}) async-start(), calls=%async_computation.1 | async-start | bytes 5160960 | tf_op jit(solution)/shard_map/all_gather | solution.py:206
  63.4 25.3 %collective-permute-start.8 = (bf16[4,2592,192]{1,2,0:T(8,128)(2,1)}, bf16[4,2592,192]{1,2,0:T(8,128)(2,1)}, u32[]{:S(2)}, u32[]{:S(2)}) collective-permute-start(bf16[4,2592,192]{1,2,0:T(8,128)(2,1)} %all-gather.3.cloned.1.call-done), channel_id=1, source_target_pairs={{0,4},{4,0},{8,12},{12,8},{16,20},{20,16},{24,28},{28,24},{32,36},... | collective-permute-start | bytes 11943944 | tf_op jit(solution)/shard_map/ppermute | solution.py:207
  64.1 7.1 collective-permute-start.2
  64.7 6.6 collective-permute-start.6
  65.7 19.8 %collective-permute-start = (f32[2,2,1,8,192]{4,3,2,1,0:T(8,128)S(1)}, f32[2,2,1,8,192]{4,3,2,1,0:T(8,128)S(1)}, u32[]{:S(2)}, u32[]{:S(2)}) collective-permute-start(f32[2,2,1,8,192]{4,3,2,1,0:T(8,128)S(1)} %get-tuple-element.602), channel_id=1, source_target_pairs={{0,4},{4,8},{8,12},{12,16},{16,20},{20,24},{24,28},{28,32},{32,36}... | collective-permute-start | bytes 73736 | tf_op jit(solution)/shard_map/ppermute | solution.py:41
  67.6 17.9 %collective-permute-start.1 = (f32[2,2,1,8,192]{4,3,2,1,0:T(8,128)S(1)}, f32[2,2,1,8,192]{4,3,2,1,0:T(8,128)S(1)}, u32[]{:S(2)}, u32[]{:S(2)}) collective-permute-start(f32[2,2,1,8,192]{4,3,2,1,0:T(8,128)S(1)} %get-tuple-element.603), channel_id=1, source_target_pairs={{4,0},{8,4},{12,8},{16,12},{20,16},{24,20},{28,24},{32,28},{36,32}... | collective-permute-start | bytes 73736 | tf_op jit(solution)/shard_map/ppermute | solution.py:42
  71.4 8.8 %collective-permute-start.7 = (f32[4,2,192]{2,1,0:T(2,128)S(1)}, f32[4,2,192]{2,1,0:T(2,128)S(1)}, u32[]{:S(2)}, u32[]{:S(2)}) collective-permute-start(f32[4,2,192]{2,1,0:T(2,128)S(1)} %constant_dynamic-update-slice_fusion.14), channel_id=1, source_target_pairs={{0,128},{64,192},{128,0},{192,64},{1,129},{65,193},{129,1},{193,65... | collective-permute-start | bytes 18440 | tf_op jit(solution)/shard_map/ppermute | solution.py:195
  134.8 54.5 %collective-permute-start.35 = (bf16[4,2592,192]{1,2,0:T(8,128)(2,1)}, bf16[4,2592,192]{1,2,0:T(8,128)(2,1)}, u32[]{:S(2)}, u32[]{:S(2)}) collective-permute-start(bf16[4,2592,192]{1,2,0:T(8,128)(2,1)} %all-gather.5.cloned.1.call-done), channel_id=1, source_target_pairs={{0,4},{4,0},{8,12},{12,8},{16,20},{20,16},{24,28},{28,24},{32,36},... | collective-permute-start | bytes 11943944 | tf_op jit(solution)/shard_map/ppermute | solution.py:207
  139.5 7.4 %collective-permute-start.20 = (f32[16,2,2,32]{3,2,1,0:T(2,128)S(1)}, f32[16,2,2,32]{3,2,1,0:T(2,128)S(1)}, u32[]{:S(2)}, u32[]{:S(2)}) collective-permute-start(f32[16,2,2,32]{3,2,1,0:T(2,128)S(1)} %add.566), channel_id=1, source_target_pairs={{0,32},{4,36},{8,40},{12,44},{16,48},{20,52},{24,56},{28,60},{32,0... | collective-permute-start | bytes 24584 | tf_op jit(solution)/shard_map/ppermute | solution.py:25
  162.5 7.4 %collective-permute-start.25 = (f32[16,2,2,32]{3,2,1,0:T(2,128)S(1)}, f32[16,2,2,32]{3,2,1,0:T(2,128)S(1)}, u32[]{:S(2)}, u32[]{:S(2)}) collective-permute-start(f32[16,2,2,32]{3,2,1,0:T(2,128)S(1)} %add.573), channel_id=1, source_target_pairs={{0,16},{4,20},{8,24},{12,28},{16,0},{20,4},{24,8},{28,12},{32,48},... | collective-permute-start | bytes 24584 | tf_op jit(solution)/shard_map/ppermute | solution.py:25
  193.2 9.7 %collective-permute-start.33 = (f32[16,2,2,32]{3,2,1,0:T(2,128)S(1)}, f32[16,2,2,32]{3,2,1,0:T(2,128)S(1)}, u32[]{:S(2)}, u32[]{:S(2)}) collective-permute-start(f32[16,2,2,32]{3,2,1,0:T(2,128)S(1)} %add.582), channel_id=1, source_target_pairs={{0,16},{4,20},{8,24},{12,28},{16,0},{20,4},{24,8},{28,12},{32,48},... | collective-permute-start | bytes 24584 | tf_op jit(solution)/shard_map/ppermute | solution.py:25
  202.9 6.9 collective-permute-start.34
  221.1 13.0 %collective-permute-start.28 = (bf16[2,2,1,8,192]{4,3,2,1,0:T(8,128)(2,1)S(1)}, bf16[2,2,1,8,192]{4,3,2,1,0:T(8,128)(2,1)S(1)}, u32[]{:S(2)}, u32[]{:S(2)}) collective-permute-start(bf16[2,2,1,8,192]{4,3,2,1,0:T(8,128)(2,1)S(1)} %get-tuple-element.587), channel_id=1, source_target_pairs={{4,0},{8,4},{12,8},{16,12},{20,16},{24,20},{28,24},{32,28},{36,32}... | collective-permute-start | bytes 36872 | tf_op jit(solution)/shard_map/ppermute | solution.py:42
  224.8 31.4 %collective-permute-start.27 = (bf16[2,2,1,8,192]{4,3,2,1,0:T(8,128)(2,1)}, bf16[2,2,1,8,192]{4,3,2,1,0:T(8,128)(2,1)}, u32[]{:S(2)}, u32[]{:S(2)}) collective-permute-start(bf16[2,2,1,8,192]{4,3,2,1,0:T(8,128)(2,1)} %get-tuple-element.586), channel_id=1, source_target_pairs={{0,4},{4,8},{8,12},{12,16},{16,20},{20,24},{24,28},{28,32},{32,36}... | collective-permute-start | bytes 36872 | tf_op jit(solution)/shard_map/ppermute | solution.py:41
  228.8 7.3 collective-permute-start.40
  236.1 9.5 %collective-permute-start.41 = (f32[16,2,2,32]{3,2,1,0:T(2,128)S(1)}, f32[16,2,2,32]{3,2,1,0:T(2,128)S(1)}, u32[]{:S(2)}, u32[]{:S(2)}) collective-permute-start(f32[16,2,2,32]{3,2,1,0:T(2,128)S(1)} %add.592), channel_id=1, source_target_pairs={{0,32},{4,36},{8,40},{12,44},{16,48},{20,52},{24,56},{28,60},{32,0... | collective-permute-start | bytes 24584 | tf_op jit(solution)/shard_map/ppermute | solution.py:25
  261.4 7.4 collective-permute-start.46
  288.7 11.5 %collective-permute-start.48 = (f32[16,2,2,32]{3,2,1,0:T(2,128)S(1)}, f32[16,2,2,32]{3,2,1,0:T(2,128)S(1)}, u32[]{:S(2)}, u32[]{:S(2)}) collective-permute-start(f32[16,2,2,32]{3,2,1,0:T(2,128)S(1)} %constant_dynamic-update-slice_fusion.1), channel_id=1, source_target_pairs={{0,4},{4,0},{8,12},{12,8},{16,20},{20,16},{24,28},{28,24},{32,36},... | collective-permute-start | bytes 24584 | tf_op jit(solution)/shard_map/ppermute | solution.py:25
  300.1 8.1 %collective-permute-start.49 = (f32[16,2,2,32]{3,2,1,0:T(2,128)S(1)}, f32[16,2,2,32]{3,2,1,0:T(2,128)S(1)}, u32[]{:S(2)}, u32[]{:S(2)}) collective-permute-start(f32[16,2,2,32]{3,2,1,0:T(2,128)S(1)} %constant_dynamic-update-slice_fusion), channel_id=1, source_target_pairs={{0,8},{4,12},{8,0},{12,4},{16,24},{20,28},{24,16},{28,20},{32,40},... | collective-permute-start | bytes 24584 | tf_op jit(solution)/shard_map/ppermute | solution.py:25
  308.2 12.1 %collective-permute-start.50 = (f32[16,2,2,32]{3,2,1,0:T(2,128)S(1)}, f32[16,2,2,32]{3,2,1,0:T(2,128)S(1)}, u32[]{:S(2)}, u32[]{:S(2)}) collective-permute-start(f32[16,2,2,32]{3,2,1,0:T(2,128)S(1)} %add.609), channel_id=1, source_target_pairs={{0,16},{4,20},{8,24},{12,28},{16,0},{20,4},{24,8},{28,12},{32,48},... | collective-permute-start | bytes 24584 | tf_op jit(solution)/shard_map/ppermute | solution.py:25
  320.3 13.9 %collective-permute-start.51 = (f32[16,2,2,32]{3,2,1,0:T(2,128)S(1)}, f32[16,2,2,32]{3,2,1,0:T(2,128)S(1)}, u32[]{:S(2)}, u32[]{:S(2)}) collective-permute-start(f32[16,2,2,32]{3,2,1,0:T(2,128)S(1)} %add.610), channel_id=1, source_target_pairs={{0,32},{4,36},{8,40},{12,44},{16,48},{20,52},{24,56},{28,60},{32,0... | collective-permute-start | bytes 24584 | tf_op jit(solution)/shard_map/ppermute | solution.py:25
  338.4 12.6 %collective-permute-start.54 = (f32[2,2,32]{2,1,0:T(2,128)S(1)}, f32[2,2,32]{2,1,0:T(2,128)S(1)}, u32[]{:S(2)}, u32[]{:S(2)}) collective-permute-start(f32[2,2,32]{2,1,0:T(2,128)S(1)} %pad_maximum_fusion.42), channel_id=1, source_target_pairs={{0,4},{4,0},{8,12},{12,8},{16,20},{20,16},{24,28},{28,24},{32,36},... | collective-permute-start | bytes 1544 | tf_op jit(solution)/shard_map/ppermute | solution.py:25
  355.4 6.8 collective-permute-start.56
  356.6 15.3 %collective-permute-start.100 = (f32[2,2,1,8,192]{4,3,2,1,0:T(8,128)}, f32[2,2,1,8,192]{4,3,2,1,0:T(8,128)}, u32[]{:S(2)}, u32[]{:S(2)}) collective-permute-start(f32[2,2,1,8,192]{4,3,2,1,0:T(8,128)} %get-tuple-element.96), channel_id=1, source_target_pairs={{0,4},{4,8},{8,12},{12,16},{16,20},{20,24},{24,28},{28,32},{32,36}... | collective-permute-start | bytes 73736 | tf_op jit(solution)/shard_map/ppermute | solution.py:41
  358.6 13.4 %collective-permute-start.101 = (f32[2,2,1,8,192]{4,3,2,1,0:T(8,128)}, f32[2,2,1,8,192]{4,3,2,1,0:T(8,128)}, u32[]{:S(2)}, u32[]{:S(2)}) collective-permute-start(f32[2,2,1,8,192]{4,3,2,1,0:T(8,128)} %get-tuple-element.97), channel_id=1, source_target_pairs={{4,0},{8,4},{12,8},{16,12},{20,16},{24,20},{28,24},{32,28},{36,32}... | collective-permute-start | bytes 73736 | tf_op jit(solution)/shard_map/ppermute | solution.py:42
  362.2 7.1 collective-permute-start.57
  363.7 7.1 collective-permute-start.52
  383.0 10.7 %collective-permute-start.60 = (f32[2,2,32]{2,1,0:T(2,128)S(1)}, f32[2,2,32]{2,1,0:T(2,128)S(1)}, u32[]{:S(2)}, u32[]{:S(2)}) collective-permute-start(f32[2,2,32]{2,1,0:T(2,128)S(1)} %pad_maximum_fusion.43), channel_id=1, source_target_pairs={{0,4},{4,0},{8,12},{12,8},{16,20},{20,16},{24,28},{28,24},{32,36},... | collective-permute-start | bytes 1544 | tf_op jit(solution)/shard_map/ppermute | solution.py:25
  393.7 12.6 %collective-permute-start.61 = (f32[2,2,32]{2,1,0:T(2,128)S(1)}, f32[2,2,32]{2,1,0:T(2,128)S(1)}, u32[]{:S(2)}, u32[]{:S(2)}) collective-permute-start(f32[2,2,32]{2,1,0:T(2,128)S(1)} %fusion.234), channel_id=1, source_target_pairs={{0,8},{4,12},{8,0},{12,4},{16,24},{20,28},{24,16},{28,20},{32,40},... | collective-permute-start | bytes 1544 | tf_op jit(solution)/shard_map/ppermute | solution.py:25
  412.3 7.6 %collective-permute-start.63 = (f32[2,2,32]{2,1,0:T(2,128)S(1)}, f32[2,2,32]{2,1,0:T(2,128)S(1)}, u32[]{:S(2)}, u32[]{:S(2)}) collective-permute-start(f32[2,2,32]{2,1,0:T(2,128)S(1)} %add.625), channel_id=1, source_target_pairs={{0,32},{4,36},{8,40},{12,44},{16,48},{20,52},{24,56},{28,60},{32,0... | collective-permute-start | bytes 1544 | tf_op jit(solution)/shard_map/ppermute | solution.py:25
  431.0 9.4 %collective-permute-start.66 = (f32[2,2,32]{2,1,0:T(2,128)S(1)}, f32[2,2,32]{2,1,0:T(2,128)S(1)}, u32[]{:S(2)}, u32[]{:S(2)}) collective-permute-start(f32[2,2,32]{2,1,0:T(2,128)S(1)} %pad_maximum_fusion.44), channel_id=1, source_target_pairs={{0,4},{4,0},{8,12},{12,8},{16,20},{20,16},{24,28},{28,24},{32,36},... | collective-permute-start | bytes 1544 | tf_op jit(solution)/shard_map/ppermute | solution.py:25
  440.4 26.3 %collective-permute-start.67 = (f32[2,2,32]{2,1,0:T(2,128)S(1)}, f32[2,2,32]{2,1,0:T(2,128)S(1)}, u32[]{:S(2)}, u32[]{:S(2)}) collective-permute-start(f32[2,2,32]{2,1,0:T(2,128)S(1)} %fusion.233), channel_id=1, source_target_pairs={{0,8},{4,12},{8,0},{12,4},{16,24},{20,28},{24,16},{28,20},{32,40},... | collective-permute-start | bytes 1544 | tf_op jit(solution)/shard_map/ppermute | solution.py:25
  472.6 7.6 %collective-permute-start.69 = (f32[2,2,32]{2,1,0:T(2,128)S(1)}, f32[2,2,32]{2,1,0:T(2,128)S(1)}, u32[]{:S(2)}, u32[]{:S(2)}) collective-permute-start(f32[2,2,32]{2,1,0:T(2,128)S(1)} %add.632), channel_id=1, source_target_pairs={{0,32},{4,36},{8,40},{12,44},{16,48},{20,52},{24,56},{28,60},{32,0... | collective-permute-start | bytes 1544 | tf_op jit(solution)/shard_map/ppermute | solution.py:25
  502.1 7.3 collective-permute-start.75
  529.7 7.0 collective-permute-start.81
  588.1 7.2 collective-permute-start.93
  620.6 15.6 %collective-permute-start.102 = (f32[2,2,2,2,2,15555]{5,4,3,2,1,0:T(2,128)}, f32[2,2,2,2,2,15555]{5,4,3,2,1,0:T(2,128)}, u32[]{:S(2)}, u32[]{:S(2)}) collective-permute-start(f32[2,2,2,2,2,15555]{5,4,3,2,1,0:T(2,128)} %fusion.21), channel_id=1, source_target_pairs={{0,4},{4,0},{8,12},{12,8},{16,20},{20,16},{24,28},{28,24},{32,36},... | collective-permute-start | bytes 5973128 | tf_op jit(solution)/shard_map/ppermute | solution.py:170
  639.5 25.2 %collective-permute-start.103 = (f32[2,2,2,2,15555]{4,3,2,1,0:T(2,128)S(1)}, f32[2,2,2,2,15555]{4,3,2,1,0:T(2,128)S(1)}, u32[]{:S(2)}, u32[]{:S(2)}) collective-permute-start(f32[2,2,2,2,15555]{4,3,2,1,0:T(2,128)S(1)} %dynamic-slice_bitcast_fusion), channel_id=1, source_target_pairs={{0,8},{4,12},{8,0},{12,4},{16,24},{20,28},{24,16},{28,20},{32,40},... | collective-permute-start | bytes 2986568 | tf_op jit(solution)/shard_map/ppermute | solution.py:170
  641.7 43.9 %collective-permute-start.95 = (f32[2,2,2,2,15555]{4,3,2,1,0:T(2,128)S(1)}, f32[2,2,2,2,15555]{4,3,2,1,0:T(2,128)S(1)}, u32[]{:S(2)}, u32[]{:S(2)}) collective-permute-start(f32[2,2,2,2,15555]{4,3,2,1,0:T(2,128)S(1)} %dynamic-slice_bitcast_fusion.1), channel_id=1, source_target_pairs={{0,8},{4,12},{8,0},{12,4},{16,24},{20,28},{24,16},{28,20},{32,40},... | collective-permute-start | bytes 2986568 | tf_op jit(solution)/shard_map/ppermute | solution.py:170
  665.5 22.7 %collective-permute-start.104 = (f32[2,2,2,15555]{3,2,1,0:T(2,128)S(1)}, f32[2,2,2,15555]{3,2,1,0:T(2,128)S(1)}, u32[]{:S(2)}, u32[]{:S(2)}) collective-permute-start(f32[2,2,2,15555]{3,2,1,0:T(2,128)S(1)} %dynamic-slice_bitcast_fusion.2), channel_id=1, source_target_pairs={{0,32},{4,36},{8,40},{12,44},{16,48},{20,52},{24,56},{28,60},{32,0... | collective-permute-start | bytes 1493288 | tf_op jit(solution)/shard_map/ppermute | solution.py:170
  686.2 12.9 %collective-permute-start.96 = (f32[2,2,2,15555]{3,2,1,0:T(2,128)S(1)}, f32[2,2,2,15555]{3,2,1,0:T(2,128)S(1)}, u32[]{:S(2)}, u32[]{:S(2)}) collective-permute-start(f32[2,2,2,15555]{3,2,1,0:T(2,128)S(1)} %dynamic-slice_bitcast_fusion.3), channel_id=1, source_target_pairs={{0,32},{4,36},{8,40},{12,44},{16,48},{20,52},{24,56},{28,60},{32,0... | collective-permute-start | bytes 1493288 | tf_op jit(solution)/shard_map/ppermute | solution.py:170
  688.4 15.9 %collective-permute-start.105 = (f32[2,2,15555]{2,1,0:T(2,128)S(1)}, f32[2,2,15555]{2,1,0:T(2,128)S(1)}, u32[]{:S(2)}, u32[]{:S(2)}) collective-permute-start(f32[2,2,15555]{2,1,0:T(2,128)S(1)} %dynamic-slice_bitcast_fusion.4), channel_id=1, source_target_pairs={{0,16},{4,20},{8,24},{12,28},{16,0},{20,4},{24,8},{28,12},{32,48},... | collective-permute-start | bytes 746648 | tf_op jit(solution)/shard_map/ppermute | solution.py:170
  699.5 9.7 %collective-permute-start.97 = (f32[2,2,15555]{2,1,0:T(2,128)S(1)}, f32[2,2,15555]{2,1,0:T(2,128)S(1)}, u32[]{:S(2)}, u32[]{:S(2)}) collective-permute-start(f32[2,2,15555]{2,1,0:T(2,128)S(1)} %dynamic-slice_bitcast_fusion.5), channel_id=1, source_target_pairs={{0,16},{4,20},{8,24},{12,28},{16,0},{20,4},{24,8},{28,12},{32,48},... | collective-permute-start | bytes 746648 | tf_op jit(solution)/shard_map/ppermute | solution.py:170
  704.8 9.4 %collective-permute-start.106 = (f32[2,15555]{1,0:T(2,128)S(1)}, f32[2,15555]{1,0:T(2,128)S(1)}, u32[]{:S(2)}, u32[]{:S(2)}) collective-permute-start(f32[2,15555]{1,0:T(2,128)S(1)} %bitcast.478), channel_id=1, source_target_pairs={{0,1},{1,0},{2,3},{3,2},{4,5},{5,4},{6,7},{7,6},{8,9},{9,8},{10,11... | collective-permute-start | bytes 373328 | tf_op jit(solution)/shard_map/ppermute | solution.py:170
  709.6 13.0 %collective-permute-start.98 = (f32[2,15555]{1,0:T(2,128)S(1)}, f32[2,15555]{1,0:T(2,128)S(1)}, u32[]{:S(2)}, u32[]{:S(2)}) collective-permute-start(f32[2,15555]{1,0:T(2,128)S(1)} %bitcast.479), channel_id=1, source_target_pairs={{0,1},{1,0},{2,3},{3,2},{4,5},{5,4},{6,7},{7,6},{8,9},{9,8},{10,11... | collective-permute-start | bytes 373328 | tf_op jit(solution)/shard_map/ppermute | solution.py:170
  714.7 12.0 %collective-permute-start.107 = (f32[15555]{0:T(1024)S(1)}, f32[15555]{0:T(1024)S(1)}, u32[]{:S(2)}, u32[]{:S(2)}) collective-permute-start(f32[15555]{0:T(1024)S(1)} %get-tuple-element.25), channel_id=1, source_target_pairs={{0,2},{1,3},{2,0},{3,1},{4,6},{5,7},{6,4},{7,5},{8,10},{9,11},{10,... | collective-permute-start | bytes 186668 | tf_op jit(solution)/shard_map/ppermute | solution.py:170
  723.0 8.3 %collective-permute-start.99 = (f32[15555]{0:T(1024)S(1)}, f32[15555]{0:T(1024)S(1)}, u32[]{:S(2)}, u32[]{:S(2)}) collective-permute-start(f32[15555]{0:T(1024)S(1)} %get-tuple-element.27), channel_id=1, source_target_pairs={{0,2},{1,3},{2,0},{3,1},{4,6},{5,7},{6,4},{7,5},{8,10},{9,11},{10,... | collective-permute-start | bytes 186668 | tf_op jit(solution)/shard_map/ppermute | solution.py:170
  (165 other events, 1442.3 us)
Sparse Core Ops, SparseCore 0:
  10.3 53.0 all-gather.2
  80.2 49.9 all-gather.4

commit v3 on v2

--- a/solution.py
+++ b/solution.py
@@ -27,13 +27,6 @@
     return value
 
 
-def rows_gather(value):
-    count = lax.axis_size("rows")
-    slots = jnp.zeros((count,) + value.shape, value.dtype)
-    slots = lax.dynamic_update_index_in_dim(slots, value, lax.axis_index("rows"), 0)
-    return rows_allsum(slots)
-
-
 def edge_rows(block):
     count = lax.axis_size("rows")
     up = [(i, i + 1) for i in range(count - 1)]
@@ -41,6 +34,30 @@
     low = lax.ppermute(block[:, :, -1:], "rows", up)
     high = lax.ppermute(block[:, :, :1], "rows", down)
     return low, high
+
+
+def allsum_with_halo(value, block):
+    count = lax.axis_size("rows")
+    if count % 2 or (count & (count - 1)):
+        low, high = edge_rows(block)
+        return rows_allsum(value), low, high
+    even = lax.axis_index("rows") % 2 == 0
+    first, last = block[:, :, :1], block[:, :, -1:]
+    toward = jnp.where(even, last, first)
+    message = jnp.concatenate([value.reshape(-1), toward.reshape(-1)])
+    message = lax.ppermute(message, "rows", [(i, i ^ 1) for i in range(count)])
+    partner = message[value.size :].reshape(toward.shape)
+    value = value + message[: value.size].reshape(value.shape)
+    away = jnp.where(even, first, last)
+    swap = [(i, i + 1) for i in range(1, count - 1, 2)] + [(i + 1, i) for i in range(1, count - 1, 2)]
+    other = lax.ppermute(away, "rows", swap)
+    mask = 2
+    while mask < count:
+        value = value + lax.ppermute(value, "rows", [(i, i ^ mask) for i in range(count)])
+        mask *= 2
+    low = jnp.where(even, other, partner)
+    high = jnp.where(even, partner, other)
+    return value, low, high
 
 
 def gather_patches(grown_rows):
@@ -90,8 +107,12 @@
     local_mean = local_sum / local_count
     deviation = grouped - local_mean[:, None, :, None]
     local_sq = jnp.sum(deviation * deviation, axis=(1, 3))
-    low, high = edge_rows(volume)
-    gathered = rows_gather(jnp.stack([local_sum, local_sq]))
+    count = lax.axis_size("rows")
+    slots = jnp.zeros((count, 2) + local_sum.shape, local_sum.dtype)
+    slots = lax.dynamic_update_index_in_dim(
+        slots, jnp.stack([local_sum, local_sq]), lax.axis_index("rows"), 0
+    )
+    gathered, low, high = allsum_with_halo(slots, volume)
     sums = gathered[:, 0]
     squares = gathered[:, 1]
     centre = jnp.sum(sums, axis=0) / counted
@@ -121,9 +142,9 @@
     hat_grad = pre_grad * gain_vec
     grouped_grad = hat_grad.reshape(batches, -1, GROUPS, channels // GROUPS)
     grouped_hat = normed.reshape(batches, -1, GROUPS, channels // GROUPS)
-    halo_low, halo_high = edge_rows(jnp.concatenate([hat_grad, normed], axis=-1))
-    sums = rows_allsum(
-        jnp.stack([jnp.sum(grouped_grad, axis=(1, 3)), jnp.sum(grouped_grad * grouped_hat, axis=(1, 3))])
+    sums, halo_low, halo_high = allsum_with_halo(
+        jnp.stack([jnp.sum(grouped_grad, axis=(1, 3)), jnp.sum(grouped_grad * grouped_hat, axis=(1, 3))]),
+        jnp.concatenate([hat_grad, normed], axis=-1),
     )
     first = spread_groups(sums[0] / counted, channels)
     second = spread_groups(sums[1] / counted, channels)

time: 754 us -> 711 us (0.943)
  the two profiles are of different devices: /device:TPU:8 before, /device:TPU:96 now
where the time goes in v3:
time: 711 us; the launch traced here: 697 us
  waiting for transfers between devices  248 us (35%)
  local copies, waits for them, and re-layouts  219 us (31%)
  starting transfers between devices  110 us (15%)
  other arithmetic  57.9 us (8%)
  matrix products  44.7 us (6%)
  between operations  18.4 us (3%)
    ppermute x45, waiting for transfers between devices, allsum_with_halo(): lax.ppermute(value, 'rows', [(i, i ^ mask) for i in range(count)])  93.8 us
    ppermute x12, waiting for transfers between devices, tree_scatter(): lax.ppermute(send, axis, [(i, i ^ 1 << bit) for i in range(count)])  67.4 us
    transpose x16, local copies, waits for them, and re-layouts, flipped(): return jnp.swapaxes(blocks, 1, 2).reshape(-1, blocks.shape[1])  64.8 us
    all_gather x2, waiting for transfers between devices, section_weights(): lax.all_gather(lax.dynamic_slice_in_dim(weights, core * half, half, 0), '...  64.2 us
    concatenate x17, local copies, waits for them, and re-layouts, gather_patches(): jnp.concatenate(pieces, axis=-1)  48.8 us
    ppermute x15, starting transfers between devices, allsum_with_halo(): other = lax.ppermute(away, 'rows', swap)  43.8 us
    ppermute x45, starting transfers between devices, allsum_with_halo(): lax.ppermute(value, 'rows', [(i, i ^ mask) for i in range(count)])  42.1 us
    dot_general x15, matrix products, conv_rows(): out = jnp.dot(patches, weights, preferred_element_type=jnp.float32)  38.2 us
  transfers between devices with their start and end apart: 95, of which 48 were waited for; matrix products, arithmetic and copies ran while one was open for 29% of the time, Pallas kernels for 0%

profile of v3, /device:TPU:96, one launch (start us, length us, event | category | flops | bytes accessed | tf_op | source)
XLA Modules:
  0.0 697.4 jit_solution(6762472396962242542)
XLA Ops:
  10.2 52.2 %all-gather.3.cloned.1.call-done = bf16[4,2592,192]{1,2,0:T(8,128)(2,1)} async-done(((bf16[1,2592,192]{1,2,0:T(8,128)(2,1)}), bf16[4,2592,192]{1,2,0:T(8,128)(2,1)}) %all-gather.3.cloned.1.call-update) | async-done | bytes 3981328 | tf_op jit(solution)/shard_map/all_gather | solution.py:227
  64.6 4.4 collective-permute-start
  80.7 3.9 collective-permute-done.4
  88.7 3.9 broadcast_select_fusion.2
  92.6 5.0 pad_maximum_fusion.1
  99.4 3.7 collective-permute-start.24
  106.2 5.5 collective-permute-start.8
  112.5 12.0 %all-gather.5.cloned.1.call-done = bf16[4,2592,192]{1,2,0:T(8,128)(2,1)} async-done(((bf16[1,2592,192]{1,2,0:T(8,128)(2,1)}), bf16[4,2592,192]{1,2,0:T(8,128)(2,1)}) %all-gather.5.cloned.1.call-update) | async-done | bytes 3981328 | tf_op jit(solution)/shard_map/all_gather | solution.py:227
  161.7 3.6 concatenate.313
  169.1 5.8 broadcast_select_fusion
  175.6 7.4 %pad_maximum_fusion = (bf16[1,5184,192]{1,2,0:T(8,128)(2,1)}, bf16[1,5184,192]{1,2,0:T(8,128)(2,1)}, bf16[1,5184,192]{1,2,0:T(8,128)(2,1)}, bf16[1,5184,192]{1,2,0:T(8,128)(2,1)}) fusion(bf16[4,2592,192]{1,2,0:T(8,128)(2,1)} %get-tuple-element.77, bf16[4,2592,192]{1,2,0:T(8,128)(2,1)} %get-tuple-element.78), kind=kLoop, calls=%fused_computation.446 | loop fusion | flops 15925248 | bytes 15925248 | tf_op jit(solution)/shard_map/concatenate | solution.py:231
  183.0 4.3 copy.44
  196.2 4.3 copy.47
  218.4 4.3 copy.50
  226.5 4.3 copy.53
  236.8 3.6 reverse_bitcast_fusion.4
  240.4 4.3 copy.56
  251.5 3.6 concatenate.327
  258.9 3.6 reverse_bitcast_fusion.3
  262.6 4.3 copy.59
  270.7 4.3 copy.62
  295.3 3.8 concatenate.334
  305.7 4.6 copy.45
  310.2 4.6 copy.48
  314.8 4.5 copy.51
  319.3 4.5 copy.54
  323.8 4.5 copy.57
  328.4 4.6 copy.60
  333.0 4.6 copy.63
  337.6 4.5 copy.67
  358.7 3.7 concatenate.340
  384.9 4.4 collective-permute-start.45
  393.5 4.7 collective-permute-done.48
  419.0 4.7 collective-permute-done.53
  443.8 4.6 collective-permute-done.58
  469.2 4.4 collective-permute-done.63
  494.5 4.4 collective-permute-done.68
  520.1 4.6 collective-permute-done.73
  553.9 4.4 collective-permute-done.78
  568.9 7.3 %concatenate.391 = f32[2,2,2,2,2,2,15552]{6,5,4,3,2,1,0:T(2,128)} reshape(f32[5184,192]{1,0:T(8,128)} %fusion.269) | data formatting | bytes 7962624 | tf_op jit(solution)/shard_map/concatenate | solution.py:200
  581.4 3.8 fusion.21
  588.6 7.3 %concatenate.384 = f32[2,2,2,2,2,2,15552]{6,5,4,3,2,1,0:T(2,128)} reshape(f32[5184,192]{1,0:T(8,128)} %fusion.268) | data formatting | bytes 7962624 | tf_op jit(solution)/shard_map/concatenate | solution.py:200
  606.2 21.4 %collective-permute-done.88 = f32[2,2,2,2,15555]{4,3,2,1,0:T(2,128)S(1)} collective-permute-done((f32[2,2,2,2,15555]{4,3,2,1,0:T(2,128)S(1)}, f32[2,2,2,2,15555]{4,3,2,1,0:T(2,128)S(1)}, u32[]{:S(2)}, u32[]{:S(2)}) %collective-permute-start.88) | collective-permute-done | bytes 995552 | tf_op jit(solution)/shard_map/ppermute | solution.py:191
  628.4 19.6 %collective-permute-done.81 = f32[2,2,2,2,15555]{4,3,2,1,0:T(2,128)S(1)} collective-permute-done((f32[2,2,2,2,15555]{4,3,2,1,0:T(2,128)S(1)}, f32[2,2,2,2,15555]{4,3,2,1,0:T(2,128)S(1)}, u32[]{:S(2)}, u32[]{:S(2)}) %collective-permute-start.81) | collective-permute-done | bytes 995552 | tf_op jit(solution)/shard_map/ppermute | solution.py:191
  649.3 11.9 %collective-permute-done.82 = f32[2,2,2,15555]{3,2,1,0:T(2,128)S(1)} collective-permute-done((f32[2,2,2,15555]{3,2,1,0:T(2,128)S(1)}, f32[2,2,2,15555]{3,2,1,0:T(2,128)S(1)}, u32[]{:S(2)}, u32[]{:S(2)}) %collective-permute-start.82) | collective-permute-done | bytes 497792 | tf_op jit(solution)/shard_map/ppermute | solution.py:191
  662.5 6.8 collective-permute-done.83
  670.6 5.8 collective-permute-start.92
  684.9 4.1 collective-permute-done.85
  (1041 shorter events, 362.4 us)
Async XLA Ops:
  7.2 55.1 %all-gather.3.cloned.1.call-start = ((), (), s32[]{:S(2)}) async-start(), calls=%async_computation | async-start | bytes 5160960 | tf_op jit(solution)/shard_map/all_gather | solution.py:227
  10.1 114.3 %all-gather.5.cloned.1.call-start = ((), (), s32[]{:S(2)}) async-start(), calls=%async_computation.1 | async-start | bytes 5160960 | tf_op jit(solution)/shard_map/all_gather | solution.py:227
  62.4 26.3 %collective-permute-start.7 = (bf16[4,2592,192]{1,2,0:T(8,128)(2,1)}, bf16[4,2592,192]{1,2,0:T(8,128)(2,1)}, u32[]{:S(2)}, u32[]{:S(2)}) collective-permute-start(bf16[4,2592,192]{1,2,0:T(8,128)(2,1)} %all-gather.3.cloned.1.call-done), channel_id=1, source_target_pairs={{0,4},{4,0},{8,12},{12,8},{16,20},{20,16},{24,28},{28,24},{32,36},... | collective-permute-start | bytes 11943944 | tf_op jit(solution)/shard_map/ppermute | solution.py:228
  62.4 6.6 collective-permute-start.5
  64.3 6.6 collective-permute-start.1
  64.6 16.1 %collective-permute-start = (f32[2,2,1,8,192]{4,3,2,1,0:T(8,128)S(1)}, f32[2,2,1,8,192]{4,3,2,1,0:T(8,128)S(1)}, u32[]{:S(2)}, u32[]{:S(2)}) collective-permute-start(f32[2,2,1,8,192]{4,3,2,1,0:T(8,128)S(1)} %get-tuple-element.117), channel_id=1, source_target_pairs={{4,8},{12,16},{20,24},{28,32},{36,40},{44,48},{52,56},{8,4},{16,12... | collective-permute-start | bytes 73736 | tf_op jit(solution)/shard_map/ppermute | solution.py:53
  99.4 6.2 collective-permute-start.24
  103.2 8.7 %collective-permute-start.23 = (bf16[2,2,1,8,192]{4,3,2,1,0:T(8,128)(2,1)S(1)}, bf16[2,2,1,8,192]{4,3,2,1,0:T(8,128)(2,1)S(1)}, u32[]{:S(2)}, u32[]{:S(2)}) collective-permute-start(bf16[2,2,1,8,192]{4,3,2,1,0:T(8,128)(2,1)S(1)} %get-tuple-element.611), channel_id=1, source_target_pairs={{0,4},{4,8},{8,12},{12,16},{16,20},{20,24},{24,28},{28,32},{32,36}... | collective-permute-start | bytes 36872 | tf_op jit(solution)/shard_map/ppermute | solution.py:34
  105.3 6.5 collective-permute-start.10
  106.2 19.1 %collective-permute-start.8 = (f32[2,2,1,8,192]{4,3,2,1,0:T(8,128)S(1)}, f32[2,2,1,8,192]{4,3,2,1,0:T(8,128)S(1)}, u32[]{:S(2)}, u32[]{:S(2)}) collective-permute-start(f32[2,2,1,8,192]{4,3,2,1,0:T(8,128)S(1)} %get-tuple-element.115), channel_id=1, source_target_pairs={{4,8},{12,16},{20,24},{28,32},{36,40},{44,48},{52,56},{8,4},{16,12... | collective-permute-start | bytes 73736 | tf_op jit(solution)/shard_map/ppermute | solution.py:53
  111.8 12.8 %collective-permute-start.11 = (f32[16,2,2,32]{3,2,1,0:T(2,128)S(1)}, f32[16,2,2,32]{3,2,1,0:T(2,128)S(1)}, u32[]{:S(2)}, u32[]{:S(2)}) collective-permute-start(f32[16,2,2,32]{3,2,1,0:T(2,128)S(1)} %add.572), channel_id=1, source_target_pairs={{0,16},{4,20},{8,24},{12,28},{16,0},{20,4},{24,8},{28,12},{32,48},... | collective-permute-start | bytes 24584 | tf_op jit(solution)/shard_map/ppermute | solution.py:56
  124.5 44.6 %collective-permute-start.30 = (bf16[4,2592,192]{1,2,0:T(8,128)(2,1)}, bf16[4,2592,192]{1,2,0:T(8,128)(2,1)}, u32[]{:S(2)}, u32[]{:S(2)}) collective-permute-start(bf16[4,2592,192]{1,2,0:T(8,128)(2,1)} %all-gather.5.cloned.1.call-done), channel_id=1, source_target_pairs={{0,4},{4,0},{8,12},{12,8},{16,20},{20,16},{24,28},{28,24},{32,36},... | collective-permute-start | bytes 11943944 | tf_op jit(solution)/shard_map/ppermute | solution.py:228
  142.7 12.7 %collective-permute-start.13 = (f32[2,2,1,8,192]{4,3,2,1,0:T(8,128)}, f32[2,2,1,8,192]{4,3,2,1,0:T(8,128)}, u32[]{:S(2)}, u32[]{:S(2)}) collective-permute-start(f32[2,2,1,8,192]{4,3,2,1,0:T(8,128)} %get-tuple-element.113), channel_id=1, source_target_pairs={{4,8},{12,16},{20,24},{28,32},{36,40},{44,48},{52,56},{8,4},{16,12... | collective-permute-start | bytes 73736 | tf_op jit(solution)/shard_map/ppermute | solution.py:53
  146.7 7.3 %collective-permute-start.16 = (f32[16,2,2,32]{3,2,1,0:T(2,128)}, f32[16,2,2,32]{3,2,1,0:T(2,128)}, u32[]{:S(2)}, u32[]{:S(2)}) collective-permute-start(f32[16,2,2,32]{3,2,1,0:T(2,128)} %add.580), channel_id=1, source_target_pairs={{0,16},{4,20},{8,24},{12,28},{16,0},{20,4},{24,8},{28,12},{32,48},... | collective-permute-start | bytes 24584 | tf_op jit(solution)/shard_map/ppermute | solution.py:56
  174.9 15.1 %collective-permute-start.20 = (f32[16,2,2,32]{3,2,1,0:T(2,128)S(1)}, f32[16,2,2,32]{3,2,1,0:T(2,128)S(1)}, u32[]{:S(2)}, u32[]{:S(2)}) collective-permute-start(f32[16,2,2,32]{3,2,1,0:T(2,128)S(1)} %constant_dynamic-update-slice_fusion.8), channel_id=1, source_target_pairs={{0,8},{4,12},{8,0},{12,4},{16,24},{20,28},{24,16},{28,20},{32,40},... | collective-permute-start | bytes 24584 | tf_op jit(solution)/shard_map/ppermute | solution.py:56
  187.3 14.1 %collective-permute-start.18 = (f32[2,2,1,8,192]{4,3,2,1,0:T(8,128)S(1)}, f32[2,2,1,8,192]{4,3,2,1,0:T(8,128)S(1)}, u32[]{:S(2)}, u32[]{:S(2)}) collective-permute-start(f32[2,2,1,8,192]{4,3,2,1,0:T(8,128)S(1)} %get-tuple-element.111), channel_id=1, source_target_pairs={{4,8},{12,16},{20,24},{28,32},{36,40},{44,48},{52,56},{8,4},{16,12... | collective-permute-start | bytes 73736 | tf_op jit(solution)/shard_map/ppermute | solution.py:53
  190.1 10.5 %collective-permute-start.21 = (f32[16,2,2,32]{3,2,1,0:T(2,128)S(1)}, f32[16,2,2,32]{3,2,1,0:T(2,128)S(1)}, u32[]{:S(2)}, u32[]{:S(2)}) collective-permute-start(f32[16,2,2,32]{3,2,1,0:T(2,128)S(1)} %add.588), channel_id=1, source_target_pairs={{0,16},{4,20},{8,24},{12,28},{16,0},{20,4},{24,8},{28,12},{32,48},... | collective-permute-start | bytes 24584 | tf_op jit(solution)/shard_map/ppermute | solution.py:56
  214.8 8.0 %collective-permute-start.26 = (f32[8192]{0:T(1024)S(1)}, f32[8192]{0:T(1024)S(1)}, u32[]{:S(2)}, u32[]{:S(2)}) collective-permute-start(f32[8192]{0:T(1024)S(1)} %pad_maximum_fusion.53), channel_id=1, source_target_pairs={{0,4},{4,0},{8,12},{12,8},{16,20},{20,16},{24,28},{28,24},{32,36},... | collective-permute-start | bytes 98312 | tf_op jit(solution)/shard_map/ppermute | solution.py:48
  222.9 11.4 %collective-permute-start.27 = (f32[16,2,2,32]{3,2,1,0:T(2,128)S(1)}, f32[16,2,2,32]{3,2,1,0:T(2,128)S(1)}, u32[]{:S(2)}, u32[]{:S(2)}) collective-permute-start(f32[16,2,2,32]{3,2,1,0:T(2,128)S(1)} %constant_dynamic-update-slice_fusion.6), channel_id=1, source_target_pairs={{0,8},{4,12},{8,0},{12,4},{16,24},{20,28},{24,16},{28,20},{32,40},... | collective-permute-start | bytes 24584 | tf_op jit(solution)/shard_map/ppermute | solution.py:56
  230.8 14.5 %collective-permute-start.25 = (f32[2,2,1,8,192]{4,3,2,1,0:T(8,128)S(1)}, f32[2,2,1,8,192]{4,3,2,1,0:T(8,128)S(1)}, u32[]{:S(2)}, u32[]{:S(2)}) collective-permute-start(f32[2,2,1,8,192]{4,3,2,1,0:T(8,128)S(1)} %get-tuple-element.109), channel_id=1, source_target_pairs={{4,8},{12,16},{20,24},{28,32},{36,40},{44,48},{52,56},{8,4},{16,12... | collective-permute-start | bytes 73736 | tf_op jit(solution)/shard_map/ppermute | solution.py:53
  234.3 10.5 %collective-permute-start.28 = (f32[16,2,2,32]{3,2,1,0:T(2,128)S(1)}, f32[16,2,2,32]{3,2,1,0:T(2,128)S(1)}, u32[]{:S(2)}, u32[]{:S(2)}) collective-permute-start(f32[16,2,2,32]{3,2,1,0:T(2,128)S(1)} %add.597), channel_id=1, source_target_pairs={{0,16},{4,20},{8,24},{12,28},{16,0},{20,4},{24,8},{28,12},{32,48},... | collective-permute-start | bytes 24584 | tf_op jit(solution)/shard_map/ppermute | solution.py:56
  258.8 8.1 %collective-permute-start.32 = (f32[8192]{0:T(1024)S(1)}, f32[8192]{0:T(1024)S(1)}, u32[]{:S(2)}, u32[]{:S(2)}) collective-permute-start(f32[8192]{0:T(1024)S(1)} %pad_maximum_fusion.54), channel_id=1, source_target_pairs={{0,4},{4,0},{8,12},{12,8},{16,20},{20,16},{24,28},{28,24},{32,36},... | collective-permute-start | bytes 98312 | tf_op jit(solution)/shard_map/ppermute | solution.py:48
  267.0 11.1 %collective-permute-start.33 = (f32[16,2,2,32]{3,2,1,0:T(2,128)S(1)}, f32[16,2,2,32]{3,2,1,0:T(2,128)S(1)}, u32[]{:S(2)}, u32[]{:S(2)}) collective-permute-start(f32[16,2,2,32]{3,2,1,0:T(2,128)S(1)} %constant_dynamic-update-slice_fusion.4), channel_id=1, source_target_pairs={{0,8},{4,12},{8,0},{12,4},{16,24},{20,28},{24,16},{28,20},{32,40},... | collective-permute-start | bytes 24584 | tf_op jit(solution)/shard_map/ppermute | solution.py:56
  275.0 14.0 %collective-permute-start.31 = (f32[2,2,1,8,192]{4,3,2,1,0:T(8,128)S(1)}, f32[2,2,1,8,192]{4,3,2,1,0:T(8,128)S(1)}, u32[]{:S(2)}, u32[]{:S(2)}) collective-permute-start(f32[2,2,1,8,192]{4,3,2,1,0:T(8,128)S(1)} %get-tuple-element.107), channel_id=1, source_target_pairs={{4,8},{12,16},{20,24},{28,32},{36,40},{44,48},{52,56},{8,4},{16,12... | collective-permute-start | bytes 73736 | tf_op jit(solution)/shard_map/ppermute | solution.py:53
  278.1 9.9 %collective-permute-start.34 = (f32[16,2,2,32]{3,2,1,0:T(2,128)S(1)}, f32[16,2,2,32]{3,2,1,0:T(2,128)S(1)}, u32[]{:S(2)}, u32[]{:S(2)}) collective-permute-start(f32[16,2,2,32]{3,2,1,0:T(2,128)S(1)} %add.606), channel_id=1, source_target_pairs={{0,16},{4,20},{8,24},{12,28},{16,0},{20,4},{24,8},{28,12},{32,48},... | collective-permute-start | bytes 24584 | tf_op jit(solution)/shard_map/ppermute | solution.py:56
  302.1 40.0 %collective-permute-start.37 = (f32[8192]{0:T(1024)S(1)}, f32[8192]{0:T(1024)S(1)}, u32[]{:S(2)}, u32[]{:S(2)}) collective-permute-start(f32[8192]{0:T(1024)S(1)} %pad_maximum_fusion.55), channel_id=1, source_target_pairs={{0,4},{4,0},{8,12},{12,8},{16,20},{20,16},{24,28},{28,24},{32,36},... | collective-permute-start | bytes 98312 | tf_op jit(solution)/shard_map/ppermute | solution.py:48
  343.0 9.6 %collective-permute-start.36 = (f32[2,2,1,8,192]{4,3,2,1,0:T(8,128)S(1)}, f32[2,2,1,8,192]{4,3,2,1,0:T(8,128)S(1)}, u32[]{:S(2)}, u32[]{:S(2)}) collective-permute-start(f32[2,2,1,8,192]{4,3,2,1,0:T(8,128)S(1)} %get-tuple-element.105), channel_id=1, source_target_pairs={{4,8},{12,16},{20,24},{28,32},{36,40},{44,48},{52,56},{8,4},{16,12... | collective-permute-start | bytes 73736 | tf_op jit(solution)/shard_map/ppermute | solution.py:53
  377.2 7.7 %collective-permute-start.86 = (f32[2,2,1,8,192]{4,3,2,1,0:T(8,128)S(1)}, f32[2,2,1,8,192]{4,3,2,1,0:T(8,128)S(1)}, u32[]{:S(2)}, u32[]{:S(2)}) collective-permute-start(f32[2,2,1,8,192]{4,3,2,1,0:T(8,128)S(1)} %get-tuple-element.103), channel_id=1, source_target_pairs={{4,8},{12,16},{20,24},{28,32},{36,40},{44,48},{52,56},{8,4},{16,12... | collective-permute-start | bytes 73736 | tf_op jit(solution)/shard_map/ppermute | solution.py:53
  384.9 7.5 %collective-permute-start.45 = (f32[2,2,1,8,384]{4,3,2,1,0:T(8,128)S(1)}, f32[2,2,1,8,384]{4,3,2,1,0:T(8,128)S(1)}, u32[]{:S(2)}, u32[]{:S(2)}) collective-permute-start(f32[2,2,1,8,384]{4,3,2,1,0:T(8,128)S(1)} %get-tuple-element.69), channel_id=1, source_target_pairs={{4,8},{12,16},{20,24},{28,32},{36,40},{44,48},{52,56},{8,4},{16,12... | collective-permute-start | bytes 147464 | tf_op jit(solution)/shard_map/ppermute | solution.py:53
  411.0 7.5 %collective-permute-start.50 = (f32[2,2,1,8,384]{4,3,2,1,0:T(8,128)S(1)}, f32[2,2,1,8,384]{4,3,2,1,0:T(8,128)S(1)}, u32[]{:S(2)}, u32[]{:S(2)}) collective-permute-start(f32[2,2,1,8,384]{4,3,2,1,0:T(8,128)S(1)} %get-tuple-element.65), channel_id=1, source_target_pairs={{4,8},{12,16},{20,24},{28,32},{36,40},{44,48},{52,56},{8,4},{16,12... | collective-permute-start | bytes 147464 | tf_op jit(solution)/shard_map/ppermute | solution.py:53
  435.7 7.5 %collective-permute-start.55 = (f32[2,2,1,8,384]{4,3,2,1,0:T(8,128)S(1)}, f32[2,2,1,8,384]{4,3,2,1,0:T(8,128)S(1)}, u32[]{:S(2)}, u32[]{:S(2)}) collective-permute-start(f32[2,2,1,8,384]{4,3,2,1,0:T(8,128)S(1)} %get-tuple-element.61), channel_id=1, source_target_pairs={{4,8},{12,16},{20,24},{28,32},{36,40},{44,48},{52,56},{8,4},{16,12... | collective-permute-start | bytes 147464 | tf_op jit(solution)/shard_map/ppermute | solution.py:53
  460.9 7.5 %collective-permute-start.60 = (f32[2,2,1,8,384]{4,3,2,1,0:T(8,128)S(1)}, f32[2,2,1,8,384]{4,3,2,1,0:T(8,128)S(1)}, u32[]{:S(2)}, u32[]{:S(2)}) collective-permute-start(f32[2,2,1,8,384]{4,3,2,1,0:T(8,128)S(1)} %get-tuple-element.57), channel_id=1, source_target_pairs={{4,8},{12,16},{20,24},{28,32},{36,40},{44,48},{52,56},{8,4},{16,12... | collective-permute-start | bytes 147464 | tf_op jit(solution)/shard_map/ppermute | solution.py:53
  486.2 7.5 %collective-permute-start.65 = (f32[2,2,1,8,384]{4,3,2,1,0:T(8,128)S(1)}, f32[2,2,1,8,384]{4,3,2,1,0:T(8,128)S(1)}, u32[]{:S(2)}, u32[]{:S(2)}) collective-permute-start(f32[2,2,1,8,384]{4,3,2,1,0:T(8,128)S(1)} %get-tuple-element.53), channel_id=1, source_target_pairs={{4,8},{12,16},{20,24},{28,32},{36,40},{44,48},{52,56},{8,4},{16,12... | collective-permute-start | bytes 147464 | tf_op jit(solution)/shard_map/ppermute | solution.py:53
  512.0 7.5 %collective-permute-start.70 = (f32[2,2,1,8,384]{4,3,2,1,0:T(8,128)S(1)}, f32[2,2,1,8,384]{4,3,2,1,0:T(8,128)S(1)}, u32[]{:S(2)}, u32[]{:S(2)}) collective-permute-start(f32[2,2,1,8,384]{4,3,2,1,0:T(8,128)S(1)} %get-tuple-element.49), channel_id=1, source_target_pairs={{4,8},{12,16},{20,24},{28,32},{36,40},{44,48},{52,56},{8,4},{16,12... | collective-permute-start | bytes 147464 | tf_op jit(solution)/shard_map/ppermute | solution.py:53
  537.7 8.7 %collective-permute-start.76 = (f32[12416]{0:T(1024)}, f32[12416]{0:T(1024)}, u32[]{:S(2)}, u32[]{:S(2)}) collective-permute-start(f32[12416]{0:T(1024)} %pad_maximum_fusion.34), channel_id=1, source_target_pairs={{0,4},{4,0},{8,12},{12,8},{16,20},{20,16},{24,28},{28,24},{32,36},... | collective-permute-start | bytes 149000 | tf_op jit(solution)/shard_map/ppermute | solution.py:48
  544.5 7.8 %collective-permute-start.75 = (f32[2,2,1,8,384]{4,3,2,1,0:T(8,128)}, f32[2,2,1,8,384]{4,3,2,1,0:T(8,128)}, u32[]{:S(2)}, u32[]{:S(2)}) collective-permute-start(f32[2,2,1,8,384]{4,3,2,1,0:T(8,128)} %get-tuple-element.45), channel_id=1, source_target_pairs={{4,8},{12,16},{20,24},{28,32},{36,40},{44,48},{52,56},{8,4},{16,12... | collective-permute-start | bytes 147464 | tf_op jit(solution)/shard_map/ppermute | solution.py:53
  547.2 6.0 collective-permute-start.77
  585.2 14.1 %collective-permute-start.87 = (f32[2,2,2,2,2,15555]{5,4,3,2,1,0:T(2,128)}, f32[2,2,2,2,2,15555]{5,4,3,2,1,0:T(2,128)}, u32[]{:S(2)}, u32[]{:S(2)}) collective-permute-start(f32[2,2,2,2,2,15555]{5,4,3,2,1,0:T(2,128)} %fusion.21), channel_id=1, source_target_pairs={{0,4},{4,0},{8,12},{12,8},{16,20},{20,16},{24,28},{28,24},{32,36},... | collective-permute-start | bytes 5973128 | tf_op jit(solution)/shard_map/ppermute | solution.py:191
  602.6 25.1 %collective-permute-start.88 = (f32[2,2,2,2,15555]{4,3,2,1,0:T(2,128)S(1)}, f32[2,2,2,2,15555]{4,3,2,1,0:T(2,128)S(1)}, u32[]{:S(2)}, u32[]{:S(2)}) collective-permute-start(f32[2,2,2,2,15555]{4,3,2,1,0:T(2,128)S(1)} %dynamic-slice_bitcast_fusion), channel_id=1, source_target_pairs={{0,8},{4,12},{8,0},{12,4},{16,24},{20,28},{24,16},{28,20},{32,40},... | collective-permute-start | bytes 2986568 | tf_op jit(solution)/shard_map/ppermute | solution.py:191
  604.4 43.6 %collective-permute-start.81 = (f32[2,2,2,2,15555]{4,3,2,1,0:T(2,128)S(1)}, f32[2,2,2,2,15555]{4,3,2,1,0:T(2,128)S(1)}, u32[]{:S(2)}, u32[]{:S(2)}) collective-permute-start(f32[2,2,2,2,15555]{4,3,2,1,0:T(2,128)S(1)} %dynamic-slice_bitcast_fusion.1), channel_id=1, source_target_pairs={{0,8},{4,12},{8,0},{12,4},{16,24},{20,28},{24,16},{28,20},{32,40},... | collective-permute-start | bytes 2986568 | tf_op jit(solution)/shard_map/ppermute | solution.py:191
  628.3 20.5 %collective-permute-start.89 = (f32[2,2,2,15555]{3,2,1,0:T(2,128)S(1)}, f32[2,2,2,15555]{3,2,1,0:T(2,128)S(1)}, u32[]{:S(2)}, u32[]{:S(2)}) collective-permute-start(f32[2,2,2,15555]{3,2,1,0:T(2,128)S(1)} %dynamic-slice_bitcast_fusion.2), channel_id=1, source_target_pairs={{0,32},{4,36},{8,40},{12,44},{16,48},{20,52},{24,56},{28,60},{32,0... | collective-permute-start | bytes 1493288 | tf_op jit(solution)/shard_map/ppermute | solution.py:191
  648.7 12.4 %collective-permute-start.82 = (f32[2,2,2,15555]{3,2,1,0:T(2,128)S(1)}, f32[2,2,2,15555]{3,2,1,0:T(2,128)S(1)}, u32[]{:S(2)}, u32[]{:S(2)}) collective-permute-start(f32[2,2,2,15555]{3,2,1,0:T(2,128)S(1)} %dynamic-slice_bitcast_fusion.3), channel_id=1, source_target_pairs={{0,32},{4,36},{8,40},{12,44},{16,48},{20,52},{24,56},{28,60},{32,0... | collective-permute-start | bytes 1493288 | tf_op jit(solution)/shard_map/ppermute | solution.py:191
  649.1 12.4 %collective-permute-start.90 = (f32[2,2,15555]{2,1,0:T(2,128)S(1)}, f32[2,2,15555]{2,1,0:T(2,128)S(1)}, u32[]{:S(2)}, u32[]{:S(2)}) collective-permute-start(f32[2,2,15555]{2,1,0:T(2,128)S(1)} %dynamic-slice_bitcast_fusion.4), channel_id=1, source_target_pairs={{0,16},{4,20},{8,24},{12,28},{16,0},{20,4},{24,8},{28,12},{32,48},... | collective-permute-start | bytes 746648 | tf_op jit(solution)/shard_map/ppermute | solution.py:191
  661.5 7.8 %collective-permute-start.83 = (f32[2,2,15555]{2,1,0:T(2,128)S(1)}, f32[2,2,15555]{2,1,0:T(2,128)S(1)}, u32[]{:S(2)}, u32[]{:S(2)}) collective-permute-start(f32[2,2,15555]{2,1,0:T(2,128)S(1)} %dynamic-slice_bitcast_fusion.5), channel_id=1, source_target_pairs={{0,16},{4,20},{8,24},{12,28},{16,0},{20,4},{24,8},{28,12},{32,48},... | collective-permute-start | bytes 746648 | tf_op jit(solution)/shard_map/ppermute | solution.py:191
  662.0 8.1 %collective-permute-start.91 = (f32[2,15555]{1,0:T(2,128)S(1)}, f32[2,15555]{1,0:T(2,128)S(1)}, u32[]{:S(2)}, u32[]{:S(2)}) collective-permute-start(f32[2,15555]{1,0:T(2,128)S(1)} %bitcast.508), channel_id=1, source_target_pairs={{0,1},{1,0},{2,3},{3,2},{4,5},{5,4},{6,7},{7,6},{8,9},{9,8},{10,11... | collective-permute-start | bytes 373328 | tf_op jit(solution)/shard_map/ppermute | solution.py:191
  669.7 10.0 %collective-permute-start.84 = (f32[2,15555]{1,0:T(2,128)S(1)}, f32[2,15555]{1,0:T(2,128)S(1)}, u32[]{:S(2)}, u32[]{:S(2)}) collective-permute-start(f32[2,15555]{1,0:T(2,128)S(1)} %bitcast.509), channel_id=1, source_target_pairs={{0,1},{1,0},{2,3},{3,2},{4,5},{5,4},{6,7},{7,6},{8,9},{9,8},{10,11... | collective-permute-start | bytes 373328 | tf_op jit(solution)/shard_map/ppermute | solution.py:191
  670.6 12.9 %collective-permute-start.92 = (f32[15555]{0:T(1024)S(1)}, f32[15555]{0:T(1024)S(1)}, u32[]{:S(2)}, u32[]{:S(2)}) collective-permute-start(f32[15555]{0:T(1024)S(1)} %get-tuple-element.25), channel_id=1, source_target_pairs={{0,2},{1,3},{2,0},{3,1},{4,6},{5,7},{6,4},{7,5},{8,10},{9,11},{10,... | collective-permute-start | bytes 186668 | tf_op jit(solution)/shard_map/ppermute | solution.py:191
  680.2 8.8 %collective-permute-start.85 = (f32[15555]{0:T(1024)S(1)}, f32[15555]{0:T(1024)S(1)}, u32[]{:S(2)}, u32[]{:S(2)}) collective-permute-start(f32[15555]{0:T(1024)S(1)} %get-tuple-element.27), channel_id=1, source_target_pairs={{0,2},{1,3},{2,0},{3,1},{4,6},{5,7},{6,4},{7,5},{8,10},{9,11},{10,... | collective-permute-start | bytes 186668 | tf_op jit(solution)/shard_map/ppermute | solution.py:191
  (171 other events, 1249.6 us)
Sparse Core Ops, SparseCore 0:
  10.3 52.0 all-gather.2
  74.2 50.2 all-gather.4

commit v4 on v2

--- a/solution.py
+++ b/solution.py
@@ -41,6 +41,41 @@
     low = lax.ppermute(block[:, :, -1:], "rows", up)
     high = lax.ppermute(block[:, :, :1], "rows", down)
     return low, high
+
+
+def gather_with_halo(value, block):
+    count = lax.axis_size("rows")
+    if count < 4 or (count & (count - 1)):
+        low, high = edge_rows(block)
+        return rows_gather(value), low, high
+    me = lax.axis_index("rows")
+    even = me % 2 == 0
+    slots = jnp.zeros((count,) + value.shape, value.dtype)
+    slots = lax.dynamic_update_index_in_dim(slots, value, me, 0)
+    filled = (jnp.arange(count) == me).astype(value.dtype)
+    first, last = block[:, :, :1], block[:, :, -1:]
+    shifted = [(i, (i + 1) % count) for i in range(1, count, 2)]
+    shifted += [((i + 1) % count, i) for i in range(1, count, 2)]
+    rounds = [([(i, i ^ 1) for i in range(count)], jnp.where(even, last, first))]
+    rounds.append((shifted, jnp.where(even, first, last)))
+    mask = 4
+    while mask < count:
+        rounds.append(([(i, i ^ mask) for i in range(count)], None))
+        mask *= 2
+    edges = []
+    for pairs, edge in rounds:
+        parts = [slots.reshape(-1), filled] + ([] if edge is None else [edge.reshape(-1)])
+        message = lax.ppermute(jnp.concatenate(parts), "rows", pairs)
+        got_slots = message[: slots.size].reshape(slots.shape)
+        got_filled = message[slots.size : slots.size + count]
+        if edge is not None:
+            edges.append(message[slots.size + count :].reshape(edge.shape))
+        keep = got_filled.reshape((count,) + (1,) * value.ndim) > 0
+        slots = jnp.where(keep, got_slots, slots)
+        filled = jnp.maximum(filled, got_filled)
+    low = jnp.where(even, edges[1], edges[0])
+    high = jnp.where(even, edges[0], edges[1])
+    return slots, low, high
 
 
 def gather_patches(grown_rows):
@@ -90,8 +125,7 @@
     local_mean = local_sum / local_count
     deviation = grouped - local_mean[:, None, :, None]
     local_sq = jnp.sum(deviation * deviation, axis=(1, 3))
-    low, high = edge_rows(volume)
-    gathered = rows_gather(jnp.stack([local_sum, local_sq]))
+    gathered, low, high = gather_with_halo(jnp.stack([local_sum, local_sq]), volume)
     sums = gathered[:, 0]
     squares = gathered[:, 1]
     centre = jnp.sum(sums, axis=0) / counted
@@ -121,10 +155,11 @@
     hat_grad = pre_grad * gain_vec
     grouped_grad = hat_grad.reshape(batches, -1, GROUPS, channels // GROUPS)
     grouped_hat = normed.reshape(batches, -1, GROUPS, channels // GROUPS)
-    halo_low, halo_high = edge_rows(jnp.concatenate([hat_grad, normed], axis=-1))
-    sums = rows_allsum(
-        jnp.stack([jnp.sum(grouped_grad, axis=(1, 3)), jnp.sum(grouped_grad * grouped_hat, axis=(1, 3))])
-    )
+    parts, halo_low, halo_high = gather_with_halo(
+        jnp.stack([jnp.sum(grouped_grad, axis=(1, 3)), jnp.sum(grouped_grad * grouped_hat, axis=(1, 3))]),
+        jnp.concatenate([hat_grad, normed], axis=-1),
+    )
+    sums = jnp.sum(parts, axis=0)
     first = spread_groups(sums[0] / counted, channels)
     second = spread_groups(sums[1] / counted, channels)
     grad_full = jnp.concatenate([halo_low[..., :channels], hat_grad, halo_high[..., :channels]], axis=2)

time: 754 us -> 727 us (0.964)
  the two profiles are of different devices: /device:TPU:8 before, /device:TPU:16 now
where the time goes in v4:
time: 727 us; the launch traced here: 713 us
  local copies, waits for them, and re-layouts  250 us (34%)
  waiting for transfers between devices  208 us (29%)
  starting transfers between devices  121 us (17%)
  other arithmetic  67.5 us (9%)
  matrix products  47 us (6%)
  between operations  19.5 us (3%)
    ppermute x60, starting transfers between devices, gather_with_halo(): message = lax.ppermute(jnp.concatenate(parts), 'rows', pairs)  85.1 us
    ppermute x60, waiting for transfers between devices, gather_with_halo(): message = lax.ppermute(jnp.concatenate(parts), 'rows', pairs)  84.4 us
    transpose x16, local copies, waits for them, and re-layouts, flipped(): return jnp.swapaxes(blocks, 1, 2).reshape(-1, blocks.shape[1])  64.8 us
    all_gather x2, waiting for transfers between devices, section_weights(): lax.all_gather(lax.dynamic_slice_in_dim(weights, core * half, half, 0), '...  64.7 us
    ppermute x12, waiting for transfers between devices, tree_scatter(): lax.ppermute(send, axis, [(i, i ^ 1 << bit) for i in range(count)])  55.3 us
    concatenate x17, local copies, waits for them, and re-layouts, gather_patches(): jnp.concatenate(pieces, axis=-1)  49.8 us
    dot_general x15, matrix products, conv_rows(): out = jnp.dot(patches, weights, preferred_element_type=jnp.float32)  40.6 us
    ppermute x12, starting transfers between devices, tree_scatter(): lax.ppermute(send, axis, [(i, i ^ 1 << bit) for i in range(count)])  27.1 us
  transfers between devices with their start and end apart: 80, of which 52 were waited for; matrix products, arithmetic and copies ran while one was open for 27% of the time, Pallas kernels for 0%

profile of v4, /device:TPU:16, one launch (start us, length us, event | category | flops | bytes accessed | tf_op | source)
XLA Modules:
  0.0 713.0 jit_solution(6344811856382194671)
XLA Ops:
  20.4 42.9 %all-gather.3.cloned.1.call-done = bf16[4,2592,192]{1,2,0:T(8,128)(2,1)} async-done(((bf16[1,2592,192]{1,2,0:T(8,128)(2,1)}), bf16[4,2592,192]{1,2,0:T(8,128)(2,1)}) %all-gather.3.cloned.1.call-update) | async-done | bytes 3981328 | tf_op jit(solution)/shard_map/all_gather | solution.py:241
  64.8 4.1 collective-permute-done.2
  76.6 3.8 broadcast_select_fusion.2
  80.4 4.9 pad_maximum_fusion.1
  117.3 4.8 collective-permute-start.13
  131.8 3.6 concatenate.457
  148.3 4.7 collective-permute-start.17
  153.6 21.9 %all-gather.5.cloned.1.call-done = bf16[4,2592,192]{1,2,0:T(8,128)(2,1)} async-done(((bf16[1,2592,192]{1,2,0:T(8,128)(2,1)}), bf16[4,2592,192]{1,2,0:T(8,128)(2,1)}) %all-gather.5.cloned.1.call-update) | async-done | bytes 3981328 | tf_op jit(solution)/shard_map/all_gather | solution.py:241
  182.5 3.6 concatenate.468
  192.5 5.8 broadcast_select_fusion.1
  198.6 3.8 collective-permute-start.23
  202.3 7.4 %fusion = (bf16[1,5184,192]{1,2,0:T(8,128)(2,1)}, bf16[1,5184,192]{1,2,0:T(8,128)(2,1)}, bf16[1,5184,192]{1,2,0:T(8,128)(2,1)}, bf16[1,5184,192]{1,2,0:T(8,128)(2,1)}) fusion(bf16[4,2592,192]{1,2,0:T(8,128)(2,1)} %get-tuple-element.81, bf16[4,2592,192]{1,2,0:T(8,128)(2,1)} %get-tuple-element.82), kind=kLoop, calls=%fused_computation.440 | loop fusion | flops 15925248 | bytes 15925248 | tf_op jit(solution)/shard_map/concatenate | solution.py:245
  216.9 3.6 concatenate.477
  232.8 3.7 concatenate.501
  236.5 4.3 copy.44
  248.8 4.3 copy.47
  260.4 3.6 concatenate.487
  271.7 4.3 copy.50
  281.6 4.3 copy.53
  288.3 3.6 reverse_bitcast_fusion.4
  291.9 4.3 copy.56
  304.1 3.7 concatenate.496
  315.2 4.3 copy.59
  320.3 3.6 reverse_bitcast_fusion.2
  323.9 4.3 copy.62
  331.4 3.6 reverse_bitcast_fusion.1
  343.9 4.5 copy.45
  348.5 4.5 copy.48
  353.0 4.5 copy.51
  357.5 4.5 copy.54
  362.1 4.5 copy.57
  366.6 4.5 copy.60
  371.1 4.5 copy.63
  375.7 4.6 copy.67
  414.4 4.3 collective-permute-start.44
  435.3 3.6 collective-permute-done.47
  439.2 5.7 collective-permute-start.48
  465.0 5.7 collective-permute-start.52
  491.0 5.9 collective-permute-start.56
  517.0 5.7 collective-permute-start.60
  582.3 7.4 %concatenate.571 = f32[2,2,2,2,2,2,15552]{6,5,4,3,2,1,0:T(2,128)} reshape(f32[5184,192]{1,0:T(8,128)} %fusion.254) | data formatting | bytes 7962624 | tf_op jit(solution)/shard_map/concatenate | solution.py:214
  594.8 3.8 fusion.21
  602.0 7.3 %concatenate.564 = f32[2,2,2,2,2,2,15552]{6,5,4,3,2,1,0:T(2,128)} reshape(f32[5184,192]{1,0:T(8,128)} %fusion.253) | data formatting | bytes 7962624 | tf_op jit(solution)/shard_map/concatenate | solution.py:214
  620.2 21.4 %collective-permute-done.73 = f32[2,2,2,2,15555]{4,3,2,1,0:T(2,128)S(1)} collective-permute-done((f32[2,2,2,2,15555]{4,3,2,1,0:T(2,128)S(1)}, f32[2,2,2,2,15555]{4,3,2,1,0:T(2,128)S(1)}, u32[]{:S(2)}, u32[]{:S(2)}) %collective-permute-start.73) | collective-permute-done | bytes 995552 | tf_op jit(solution)/shard_map/ppermute | solution.py:205
  643.8 18.5 %collective-permute-done.67 = f32[2,2,2,2,15555]{4,3,2,1,0:T(2,128)S(1)} collective-permute-done((f32[2,2,2,2,15555]{4,3,2,1,0:T(2,128)S(1)}, f32[2,2,2,2,15555]{4,3,2,1,0:T(2,128)S(1)}, u32[]{:S(2)}, u32[]{:S(2)}) %collective-permute-start.67) | collective-permute-done | bytes 995552 | tf_op jit(solution)/shard_map/ppermute | solution.py:205
  665.3 10.3 %collective-permute-done.68 = f32[2,2,2,15555]{3,2,1,0:T(2,128)S(1)} collective-permute-done((f32[2,2,2,15555]{3,2,1,0:T(2,128)S(1)}, f32[2,2,2,15555]{3,2,1,0:T(2,128)S(1)}, u32[]{:S(2)}, u32[]{:S(2)}) %collective-permute-start.68) | collective-permute-done | bytes 497792 | tf_op jit(solution)/shard_map/ppermute | solution.py:205
  687.5 3.8 collective-permute-start.77
  692.1 9.3 %collective-permute-start.71 = (f32[15555]{0:T(1024)S(1)}, f32[15555]{0:T(1024)S(1)}, u32[]{:S(2)}, u32[]{:S(2)}) collective-permute-start(f32[15555]{0:T(1024)S(1)} %get-tuple-element.27), channel_id=1, source_target_pairs={{0,2},{1,3},{2,0},{3,1},{4,6},{5,7},{6,4},{7,5},{8,10},{9,11},{10,... | collective-permute-start | bytes 186668 | tf_op jit(solution)/shard_map/ppermute | solution.py:205
  (1311 shorter events, 377.7 us)
Async XLA Ops:
  7.2 56.1 %all-gather.3.cloned.1.call-start = ((), (), s32[]{:S(2)}) async-start(), calls=%async_computation | async-start | bytes 5160960 | tf_op jit(solution)/shard_map/all_gather | solution.py:241
  10.2 165.3 %all-gather.5.cloned.1.call-start = ((), (), s32[]{:S(2)}) async-start(), calls=%async_computation.1 | async-start | bytes 5160960 | tf_op jit(solution)/shard_map/all_gather | solution.py:241
  13.5 49.8 %collective-permute-start.1 = (f32[8208]{0:T(1024)S(1)}, f32[8208]{0:T(1024)S(1)}, u32[]{:S(2)}, u32[]{:S(2)}) collective-permute-start(f32[8208]{0:T(1024)S(1)} %concatenate.431), channel_id=1, source_target_pairs={{4,8},{12,16},{20,24},{28,32},{36,40},{44,48},{52,56},{60,0},{8,4}... | collective-permute-start | bytes 98504 | tf_op jit(solution)/shard_map/ppermute | solution.py:68
  15.2 5.2 collective-permute-start.5
  63.3 13.3 %collective-permute-start.6 = (bf16[4,2592,192]{1,2,0:T(8,128)(2,1)}, bf16[4,2592,192]{1,2,0:T(8,128)(2,1)}, u32[]{:S(2)}, u32[]{:S(2)}) collective-permute-start(bf16[4,2592,192]{1,2,0:T(8,128)(2,1)} %all-gather.3.cloned.1.call-done), channel_id=1, source_target_pairs={{0,4},{4,0},{8,12},{12,8},{16,20},{20,16},{24,28},{28,24},{32,36},... | collective-permute-start | bytes 11943944 | tf_op jit(solution)/shard_map/ppermute | solution.py:242
  63.6 5.3 collective-permute-start.2
  69.2 3.8 collective-permute-start.3
  92.6 5.3 collective-permute-start.9
  98.2 4.0 collective-permute-start.10
  117.3 7.5 %collective-permute-start.13 = (f32[2064]{0:T(1024)S(1)}, f32[2064]{0:T(1024)S(1)}, u32[]{:S(2)}, u32[]{:S(2)}) collective-permute-start(f32[2064]{0:T(1024)S(1)} %pad_maximum_fusion.46), channel_id=1, source_target_pairs={{0,16},{4,20},{8,24},{12,28},{16,0},{20,4},{24,8},{28,12},{32,48},... | collective-permute-start | bytes 24776 | tf_op jit(solution)/shard_map/ppermute | solution.py:68
  139.5 4.6 collective-permute-start.15
  139.6 6.2 collective-permute-start.20
  141.6 11.5 %collective-permute-start.19 = (bf16[2,2,1,8,192]{4,3,2,1,0:T(8,128)(2,1)S(1)}, bf16[2,2,1,8,192]{4,3,2,1,0:T(8,128)(2,1)S(1)}, u32[]{:S(2)}, u32[]{:S(2)}) collective-permute-start(bf16[2,2,1,8,192]{4,3,2,1,0:T(8,128)(2,1)S(1)} %get-tuple-element.633), channel_id=1, source_target_pairs={{0,4},{4,8},{8,12},{12,16},{16,20},{20,24},{24,28},{28,32},{32,36}... | collective-permute-start | bytes 36872 | tf_op jit(solution)/shard_map/ppermute | solution.py:41
  148.3 27.2 %collective-permute-start.17 = (f32[2064]{0:T(1024)S(1)}, f32[2064]{0:T(1024)S(1)}, u32[]{:S(2)}, u32[]{:S(2)}) collective-permute-start(f32[2064]{0:T(1024)S(1)} %pad_maximum_fusion.48), channel_id=1, source_target_pairs={{0,16},{4,20},{8,24},{12,28},{16,0},{20,4},{24,8},{28,12},{32,48},... | collective-permute-start | bytes 24776 | tf_op jit(solution)/shard_map/ppermute | solution.py:68
  175.5 17.0 %collective-permute-start.25 = (bf16[4,2592,192]{1,2,0:T(8,128)(2,1)}, bf16[4,2592,192]{1,2,0:T(8,128)(2,1)}, u32[]{:S(2)}, u32[]{:S(2)}) collective-permute-start(bf16[4,2592,192]{1,2,0:T(8,128)(2,1)} %all-gather.5.cloned.1.call-done), channel_id=1, source_target_pairs={{0,4},{4,0},{8,12},{12,8},{16,20},{20,16},{24,28},{28,24},{32,36},... | collective-permute-start | bytes 11943944 | tf_op jit(solution)/shard_map/ppermute | solution.py:242
  192.1 6.2 collective-permute-start.22
  198.6 11.1 %collective-permute-start.23 = (f32[2064]{0:T(1024)S(1)}, f32[2064]{0:T(1024)S(1)}, u32[]{:S(2)}, u32[]{:S(2)}) collective-permute-start(f32[2064]{0:T(1024)S(1)} %pad_maximum_fusion.50), channel_id=1, source_target_pairs={{0,16},{4,20},{8,24},{12,28},{16,0},{20,4},{24,8},{28,12},{32,48},... | collective-permute-start | bytes 24776 | tf_op jit(solution)/shard_map/ppermute | solution.py:68
  231.6 9.2 %collective-permute-start.27 = (f32[8208]{0:T(1024)}, f32[8208]{0:T(1024)}, u32[]{:S(2)}, u32[]{:S(2)}) collective-permute-start(f32[8208]{0:T(1024)} %concatenate.480), channel_id=1, source_target_pairs={{4,8},{12,16},{20,24},{28,32},{36,40},{44,48},{52,56},{60,0},{8,4}... | collective-permute-start | bytes 98504 | tf_op jit(solution)/shard_map/ppermute | solution.py:68
  243.2 10.0 %collective-permute-start.28 = (f32[2064]{0:T(1024)S(1)}, f32[2064]{0:T(1024)S(1)}, u32[]{:S(2)}, u32[]{:S(2)}) collective-permute-start(f32[2064]{0:T(1024)S(1)} %pad_maximum_fusion.52), channel_id=1, source_target_pairs={{0,16},{4,20},{8,24},{12,28},{16,0},{20,4},{24,8},{28,12},{32,48},... | collective-permute-start | bytes 24776 | tf_op jit(solution)/shard_map/ppermute | solution.py:68
  267.8 8.3 %collective-permute-start.30 = (f32[8208]{0:T(1024)S(1)}, f32[8208]{0:T(1024)S(1)}, u32[]{:S(2)}, u32[]{:S(2)}) collective-permute-start(f32[8208]{0:T(1024)S(1)} %concatenate.488), channel_id=1, source_target_pairs={{0,4},{4,0},{8,12},{12,8},{16,20},{20,16},{24,28},{28,24},{32,36},... | collective-permute-start | bytes 98504 | tf_op jit(solution)/shard_map/ppermute | solution.py:68
  276.5 9.4 %collective-permute-start.31 = (f32[8208]{0:T(1024)S(1)}, f32[8208]{0:T(1024)S(1)}, u32[]{:S(2)}, u32[]{:S(2)}) collective-permute-start(f32[8208]{0:T(1024)S(1)} %concatenate.489), channel_id=1, source_target_pairs={{4,8},{12,16},{20,24},{28,32},{36,40},{44,48},{52,56},{60,0},{8,4}... | collective-permute-start | bytes 98504 | tf_op jit(solution)/shard_map/ppermute | solution.py:68
  286.2 10.0 %collective-permute-start.32 = (f32[2064]{0:T(1024)S(1)}, f32[2064]{0:T(1024)S(1)}, u32[]{:S(2)}, u32[]{:S(2)}) collective-permute-start(f32[2064]{0:T(1024)S(1)} %pad_maximum_fusion.54), channel_id=1, source_target_pairs={{0,16},{4,20},{8,24},{12,28},{16,0},{20,4},{24,8},{28,12},{32,48},... | collective-permute-start | bytes 24776 | tf_op jit(solution)/shard_map/ppermute | solution.py:68
  311.6 8.0 %collective-permute-start.34 = (f32[8208]{0:T(1024)S(1)}, f32[8208]{0:T(1024)S(1)}, u32[]{:S(2)}, u32[]{:S(2)}) collective-permute-start(f32[8208]{0:T(1024)S(1)} %concatenate.497), channel_id=1, source_target_pairs={{0,4},{4,0},{8,12},{12,8},{16,20},{20,16},{24,28},{28,24},{32,36},... | collective-permute-start | bytes 98504 | tf_op jit(solution)/shard_map/ppermute | solution.py:68
  320.0 8.2 %collective-permute-start.35 = (f32[8208]{0:T(1024)S(1)}, f32[8208]{0:T(1024)S(1)}, u32[]{:S(2)}, u32[]{:S(2)}) collective-permute-start(f32[8208]{0:T(1024)S(1)} %concatenate.498), channel_id=1, source_target_pairs={{4,8},{12,16},{20,24},{28,32},{36,40},{44,48},{52,56},{60,0},{8,4}... | collective-permute-start | bytes 98504 | tf_op jit(solution)/shard_map/ppermute | solution.py:68
  328.5 10.0 %collective-permute-start.36 = (f32[2064]{0:T(1024)S(1)}, f32[2064]{0:T(1024)S(1)}, u32[]{:S(2)}, u32[]{:S(2)}) collective-permute-start(f32[2064]{0:T(1024)S(1)} %pad_maximum_fusion.56), channel_id=1, source_target_pairs={{0,16},{4,20},{8,24},{12,28},{16,0},{20,4},{24,8},{28,12},{32,48},... | collective-permute-start | bytes 24776 | tf_op jit(solution)/shard_map/ppermute | solution.py:68
  338.8 41.4 %collective-permute-start.37 = (f32[2064]{0:T(1024)S(1)}, f32[2064]{0:T(1024)S(1)}, u32[]{:S(2)}, u32[]{:S(2)}) collective-permute-start(f32[2064]{0:T(1024)S(1)} %pad_maximum_fusion.57), channel_id=1, source_target_pairs={{0,32},{4,36},{8,40},{12,44},{16,48},{20,52},{24,56},{28,60},{32,0... | collective-permute-start | bytes 24776 | tf_op jit(solution)/shard_map/ppermute | solution.py:68
  390.5 5.3 collective-permute-start.40
  414.4 6.0 collective-permute-start.44
  420.7 4.2 collective-permute-start.45
  439.2 7.4 %collective-permute-start.48 = (f32[2064]{0:T(1024)S(1)}, f32[2064]{0:T(1024)S(1)}, u32[]{:S(2)}, u32[]{:S(2)}) collective-permute-start(f32[2064]{0:T(1024)S(1)} %pad_maximum_fusion.62), channel_id=1, source_target_pairs={{0,16},{4,20},{8,24},{12,28},{16,0},{20,4},{24,8},{28,12},{32,48},... | collective-permute-start | bytes 24776 | tf_op jit(solution)/shard_map/ppermute | solution.py:68
  465.0 7.4 %collective-permute-start.52 = (f32[2064]{0:T(1024)S(1)}, f32[2064]{0:T(1024)S(1)}, u32[]{:S(2)}, u32[]{:S(2)}) collective-permute-start(f32[2064]{0:T(1024)S(1)} %pad_maximum_fusion.64), channel_id=1, source_target_pairs={{0,16},{4,20},{8,24},{12,28},{16,0},{20,4},{24,8},{28,12},{32,48},... | collective-permute-start | bytes 24776 | tf_op jit(solution)/shard_map/ppermute | solution.py:68
  491.0 7.6 %collective-permute-start.56 = (f32[2064]{0:T(1024)S(1)}, f32[2064]{0:T(1024)S(1)}, u32[]{:S(2)}, u32[]{:S(2)}) collective-permute-start(f32[2064]{0:T(1024)S(1)} %pad_maximum_fusion.66), channel_id=1, source_target_pairs={{0,16},{4,20},{8,24},{12,28},{16,0},{20,4},{24,8},{28,12},{32,48},... | collective-permute-start | bytes 24776 | tf_op jit(solution)/shard_map/ppermute | solution.py:68
  517.0 7.4 %collective-permute-start.60 = (f32[2064]{0:T(1024)S(1)}, f32[2064]{0:T(1024)S(1)}, u32[]{:S(2)}, u32[]{:S(2)}) collective-permute-start(f32[2064]{0:T(1024)S(1)} %pad_maximum_fusion.68), channel_id=1, source_target_pairs={{0,16},{4,20},{8,24},{12,28},{16,0},{20,4},{24,8},{28,12},{32,48},... | collective-permute-start | bytes 24776 | tf_op jit(solution)/shard_map/ppermute | solution.py:68
  539.4 6.3 collective-permute-start.63
  551.4 9.5 %collective-permute-start.64 = (f32[2064]{0:T(1024)}, f32[2064]{0:T(1024)}, u32[]{:S(2)}, u32[]{:S(2)}) collective-permute-start(f32[2064]{0:T(1024)} %pad_maximum_fusion.70), channel_id=1, source_target_pairs={{0,16},{4,20},{8,24},{12,28},{16,0},{20,4},{24,8},{28,12},{32,48},... | collective-permute-start | bytes 24776 | tf_op jit(solution)/shard_map/ppermute | solution.py:68
  566.0 3.9 collective-permute-start.65
  598.6 14.0 %collective-permute-start.72 = (f32[2,2,2,2,2,15555]{5,4,3,2,1,0:T(2,128)}, f32[2,2,2,2,2,15555]{5,4,3,2,1,0:T(2,128)}, u32[]{:S(2)}, u32[]{:S(2)}) collective-permute-start(f32[2,2,2,2,2,15555]{5,4,3,2,1,0:T(2,128)} %fusion.21), channel_id=1, source_target_pairs={{0,4},{4,0},{8,12},{12,8},{16,20},{20,16},{24,28},{28,24},{32,36},... | collective-permute-start | bytes 5973128 | tf_op jit(solution)/shard_map/ppermute | solution.py:205
  612.0 6.6 collective-permute-start.66
  615.9 25.7 %collective-permute-start.73 = (f32[2,2,2,2,15555]{4,3,2,1,0:T(2,128)S(1)}, f32[2,2,2,2,15555]{4,3,2,1,0:T(2,128)S(1)}, u32[]{:S(2)}, u32[]{:S(2)}) collective-permute-start(f32[2,2,2,2,15555]{4,3,2,1,0:T(2,128)S(1)} %dynamic-slice_bitcast_fusion), channel_id=1, source_target_pairs={{0,8},{4,12},{8,0},{12,4},{16,24},{20,28},{24,16},{28,20},{32,40},... | collective-permute-start | bytes 2986568 | tf_op jit(solution)/shard_map/ppermute | solution.py:205
  620.1 42.1 %collective-permute-start.67 = (f32[2,2,2,2,15555]{4,3,2,1,0:T(2,128)S(1)}, f32[2,2,2,2,15555]{4,3,2,1,0:T(2,128)S(1)}, u32[]{:S(2)}, u32[]{:S(2)}) collective-permute-start(f32[2,2,2,2,15555]{4,3,2,1,0:T(2,128)S(1)} %dynamic-slice_bitcast_fusion.1), channel_id=1, source_target_pairs={{0,8},{4,12},{8,0},{12,4},{16,24},{20,28},{24,16},{28,20},{32,40},... | collective-permute-start | bytes 2986568 | tf_op jit(solution)/shard_map/ppermute | solution.py:205
  642.3 22.1 %collective-permute-start.74 = (f32[2,2,2,15555]{3,2,1,0:T(2,128)S(1)}, f32[2,2,2,15555]{3,2,1,0:T(2,128)S(1)}, u32[]{:S(2)}, u32[]{:S(2)}) collective-permute-start(f32[2,2,2,15555]{3,2,1,0:T(2,128)S(1)} %dynamic-slice_bitcast_fusion.2), channel_id=1, source_target_pairs={{0,32},{4,36},{8,40},{12,44},{16,48},{20,52},{24,56},{28,60},{32,0... | collective-permute-start | bytes 1493288 | tf_op jit(solution)/shard_map/ppermute | solution.py:205
  662.9 12.7 %collective-permute-start.68 = (f32[2,2,2,15555]{3,2,1,0:T(2,128)S(1)}, f32[2,2,2,15555]{3,2,1,0:T(2,128)S(1)}, u32[]{:S(2)}, u32[]{:S(2)}) collective-permute-start(f32[2,2,2,15555]{3,2,1,0:T(2,128)S(1)} %dynamic-slice_bitcast_fusion.3), channel_id=1, source_target_pairs={{0,32},{4,36},{8,40},{12,44},{16,48},{20,52},{24,56},{28,60},{32,0... | collective-permute-start | bytes 1493288 | tf_op jit(solution)/shard_map/ppermute | solution.py:205
  664.7 12.9 %collective-permute-start.75 = (f32[2,2,15555]{2,1,0:T(2,128)S(1)}, f32[2,2,15555]{2,1,0:T(2,128)S(1)}, u32[]{:S(2)}, u32[]{:S(2)}) collective-permute-start(f32[2,2,15555]{2,1,0:T(2,128)S(1)} %dynamic-slice_bitcast_fusion.4), channel_id=1, source_target_pairs={{0,16},{4,20},{8,24},{12,28},{16,0},{20,4},{24,8},{28,12},{32,48},... | collective-permute-start | bytes 746648 | tf_op jit(solution)/shard_map/ppermute | solution.py:205
  675.9 8.0 %collective-permute-start.69 = (f32[2,2,15555]{2,1,0:T(2,128)S(1)}, f32[2,2,15555]{2,1,0:T(2,128)S(1)}, u32[]{:S(2)}, u32[]{:S(2)}) collective-permute-start(f32[2,2,15555]{2,1,0:T(2,128)S(1)} %dynamic-slice_bitcast_fusion.5), channel_id=1, source_target_pairs={{0,16},{4,20},{8,24},{12,28},{16,0},{20,4},{24,8},{28,12},{32,48},... | collective-permute-start | bytes 746648 | tf_op jit(solution)/shard_map/ppermute | solution.py:205
  678.1 8.9 %collective-permute-start.76 = (f32[2,15555]{1,0:T(2,128)S(1)}, f32[2,15555]{1,0:T(2,128)S(1)}, u32[]{:S(2)}, u32[]{:S(2)}) collective-permute-start(f32[2,15555]{1,0:T(2,128)S(1)} %bitcast.550), channel_id=1, source_target_pairs={{0,1},{1,0},{2,3},{3,2},{4,5},{5,4},{6,7},{7,6},{8,9},{9,8},{10,11... | collective-permute-start | bytes 373328 | tf_op jit(solution)/shard_map/ppermute | solution.py:205
  684.4 7.2 %collective-permute-start.70 = (f32[2,15555]{1,0:T(2,128)S(1)}, f32[2,15555]{1,0:T(2,128)S(1)}, u32[]{:S(2)}, u32[]{:S(2)}) collective-permute-start(f32[2,15555]{1,0:T(2,128)S(1)} %bitcast.551), channel_id=1, source_target_pairs={{0,1},{1,0},{2,3},{3,2},{4,5},{5,4},{6,7},{7,6},{8,9},{9,8},{10,11... | collective-permute-start | bytes 373328 | tf_op jit(solution)/shard_map/ppermute | solution.py:205
  687.5 13.9 %collective-permute-start.77 = (f32[15555]{0:T(1024)S(1)}, f32[15555]{0:T(1024)S(1)}, u32[]{:S(2)}, u32[]{:S(2)}) collective-permute-start(f32[15555]{0:T(1024)S(1)} %get-tuple-element.25), channel_id=1, source_target_pairs={{0,2},{1,3},{2,0},{3,1},{4,6},{5,7},{6,4},{7,5},{8,10},{9,11},{10,... | collective-permute-start | bytes 186668 | tf_op jit(solution)/shard_map/ppermute | solution.py:205
  692.1 12.2 %collective-permute-start.71 = (f32[15555]{0:T(1024)S(1)}, f32[15555]{0:T(1024)S(1)}, u32[]{:S(2)}, u32[]{:S(2)}) collective-permute-start(f32[15555]{0:T(1024)S(1)} %get-tuple-element.27), channel_id=1, source_target_pairs={{0,2},{1,3},{2,0},{3,1},{4,6},{5,7},{6,4},{7,5},{8,10},{9,11},{10,... | collective-permute-start | bytes 186668 | tf_op jit(solution)/shard_map/ppermute | solution.py:205
  (152 other events, 1146.5 us)
Sparse Core Ops, SparseCore 0:
  10.3 52.9 all-gather.2
  124.9 50.5 all-gather.4
